TPU v7x, 32 devices: a whole 2x2x4 slice. The times are simulated.
32 devices in a mesh: dp: 4 (over x, core), space: 8 (over z, y).
Axes of the slice: x: 2, y: 2, z: 4, core: 2. Of those that a mesh axis runs over, the one named last changes fastest.
Arguments:
- inputs: bfloat16 [8, 4, 48, 48, 128], P('space', 'dp'), may hold values from -6 to 6
- cotangent: bfloat16 [8, 4, 48, 48, 128], P('space', 'dp'), may hold values from -6 to 6
- weight_first: bfloat16 [3, 3, 128, 128], replicated, may hold values from -0.1875 to 0.1875
- weight_second: bfloat16 [3, 3, 128, 128], replicated, may hold values from -0.1875 to 0.1875
- slot_tile: int32 [8], replicated, may hold values from 0 to 7, as said below
- neighbour_tile: int32 [8, 8], replicated, may hold values from 0 to 7, as said below
- neighbour_turns: int32 [8, 8], replicated, may hold values from 0 to 3, as said below
- corner_live: int32 [8, 4], replicated, may hold values from 0 to 1, as said below
Outputs:
- grad_inputs: bfloat16 [8, 4, 48, 48, 128], P('space', 'dp')
- grad_first: float32 [3, 3, 128, 128], replicated
- grad_second: float32 [3, 3, 128, 128], replicated
Inputs may be any that keep to these rules, and one draw needn't show every extreme that they name: `slot_tile`: a permutation of the 8 tiles; slot s is held by device s of space. A tile and each of its 8 neighbours sit at slots at most 7 apart counted around the cycle of 8 slots. `neighbour_tile`: the tables are consistent: if u is beside t in direction k with code r, then t is beside u in the opposite direction (top and bottom, left and right, top-left and bottom-right, top-right and bottom-left) with code (4 - r) % 4. No slot holds more than two of a tile's top, bottom, left and right neighbours. `neighbour_turns`: number of counterclockwise quarter turns that bring the neighbour's pixel frame into the tile's. `corner_live`: 0 where the corner pixel is missing; the tiles that meet at a vertex agree.
All inputs are finite; a program needn't handle non-finite values.
Results may differ from a plain program's by a relative error of at most 0.0049.
Values may be sent and summed in bfloat16 or wider, within the bound.
No kernel may reach another device: no remote copies, remote signals or barrier semaphores. Data moves between devices by JAX's collectives and lax.ppermute only.
A program may use at most 64 MiB of HBM per device.

v0:
```python
import math

import jax
import jax.numpy as jnp
import numpy as np
from jax import lax
from jax.sharding import PartitionSpec as P

REACH = 7

NEED_SIDE = (1, 0, 3, 2, 1, 1, 0, 0)


def side_tables():
    one = ((3, 0), (2, 0), (0, 1), (1, 1))
    side = np.zeros((4, 4), np.int32)
    flip = np.zeros((4, 4), np.int32)
    side[0] = np.arange(4)
    for r in range(1, 4):
        for s in range(4):
            s1, f1 = one[s]
            side[r, s] = side[r - 1, s1]
            flip[r, s] = flip[r - 1, s1] ^ f1
    return side, flip


def edge_rims(tile):
    return jnp.stack([tile[:, 0], tile[:, -1], tile[:, :, 0], tile[:, :, -1]])


def residues(devices):
    found = []
    for offset in range(-REACH, REACH + 1):
        res = offset % devices
        if res != 0 and res not in found:
            found.append(res)
    return found


def shift(value, by):
    length = lax.axis_size("space")
    return lax.ppermute(value, "space", [(i, (i + by) % length) for i in range(length)])


def exchange(own, offs):
    return jnp.stack([own] + [shift(own, (-o) % lax.axis_size("space")) for o in offs])


def make_plan(me, tables, devices, offs):
    slot_tile, slot_of_tile, neighbour_tile, neighbour_turns, corner_live = tables
    tile_id = slot_tile[me]
    owners = slot_of_tile[neighbour_tile[tile_id]]
    position = np.zeros((devices,), np.int32)
    for i, o in enumerate(offs):
        position[o] = i + 1
    position = jnp.asarray(position)
    from_idx = position[(owners - me) % devices]
    to_res = (owners - me) % devices
    turns = neighbour_turns[tile_id]
    side_tab, flip_tab = side_tables()
    need = jnp.asarray(np.array(NEED_SIDE, np.int32))
    sides = jnp.asarray(side_tab)[turns, need]
    flips = jnp.asarray(flip_tab)[turns, need]
    return from_idx, to_res, sides, flips, corner_live[tile_id]


def assemble(own, top, bottom, left, right, top_left, top_right, bottom_left, bottom_right):
    top_row = jnp.concatenate([top_left[:, None], top, top_right[:, None]], axis=1)
    bottom_row = jnp.concatenate([bottom_left[:, None], bottom, bottom_right[:, None]], axis=1)
    middle = jnp.concatenate([left[:, :, None], own, right[:, :, None]], axis=2)
    return jnp.concatenate([top_row[:, None], middle, bottom_row[:, None]], axis=1)


def pad_tile(tile, received, plan):
    from_idx, to_res, sides, flips, live = plan
    rows = []
    for k in range(8):
        row = received[from_idx[k], sides[k]]
        rows.append(jnp.where(flips[k] == 1, row[:, ::-1], row))
    flags = live.astype(tile.dtype)
    return assemble(
        tile,
        rows[0],
        rows[1],
        rows[2],
        rows[3],
        rows[4][:, -1] * flags[0],
        rows[5][:, 0] * flags[1],
        rows[6][:, -1] * flags[2],
        rows[7][:, 0] * flags[3],
    )


def conv_valid(padded, weight):
    return lax.conv_general_dilated(
        padded,
        weight,
        (1, 1),
        "VALID",
        dimension_numbers=("NHWC", "HWIO", "NHWC"),
        preferred_element_type=jnp.float32,
    )


def conv_full(cot, weight):
    flipped = jnp.flip(weight, (0, 1)).transpose(0, 1, 3, 2)
    return lax.conv_general_dilated(
        cot,
        flipped,
        (1, 1),
        ((2, 2), (2, 2)),
        dimension_numbers=("NHWC", "HWIO", "NHWC"),
        preferred_element_type=jnp.float32,
    )


def weight_grad(padded, cot):
    size = cot.shape[1]
    taps = []
    for di in range(3):
        row = []
        for dj in range(3):
            window = padded[:, di : di + size, dj : dj + size]
            row.append(jnp.einsum("bijc,bijd->cd", window, cot, preferred_element_type=jnp.float32))
        taps.append(jnp.stack(row))
    return jnp.stack(taps)


def send_buffers(full, plan, offs):
    from_idx, to_res, sides, flips, live = plan
    size = full.shape[1] - 2
    flags = live.astype(jnp.float32)
    rows = [full[:, 0, 1:-1], full[:, -1, 1:-1], full[:, 1:-1, 0], full[:, 1:-1, -1]]
    corners = [full[:, 0, 0] * flags[0], full[:, 0, -1] * flags[1],
               full[:, -1, 0] * flags[2], full[:, -1, -1] * flags[3]]
    ends = (size - 1, 0, size - 1, 0)
    cells = jnp.arange(size, dtype=jnp.int32)
    placed = []
    for k in range(8):
        if k < 4:
            vec = jnp.where(flips[k] == 1, rows[k][:, ::-1], rows[k])
        else:
            at = jnp.where(flips[k] == 1, size - 1 - ends[k - 4], ends[k - 4])
            vec = jnp.where((cells == at)[None, :, None], corners[k - 4][:, None, :], 0.0)
        pick = jnp.arange(4, dtype=jnp.int32) == sides[k]
        placed.append(jnp.where(pick[:, None, None, None], vec[None], 0.0))
    buffers = []
    for res in [0] + list(offs):
        total = None
        for k in range(8):
            term = jnp.where(to_res[k] == res, placed[k], 0.0)
            total = term if total is None else total + term
        buffers.append(total)
    return buffers


def return_rims(buffers, offs):
    total = buffers[0]
    for o, buf in zip(offs, buffers[1:]):
        total = total + shift(buf, o)
    return total


def add_rims(inner, total):
    inner = inner.at[:, 0].add(total[0]).at[:, -1].add(total[1])
    return inner.at[:, :, 0].add(total[2]).at[:, :, -1].add(total[3])


def xor_swap(value, axis, bit):
    size = lax.axis_size(axis)
    return lax.ppermute(value, axis, [(i, i ^ bit) for i in range(size)])


def all_reduce(flat, axes):
    stages = []
    for axis in axes:
        size = lax.axis_size(axis)
        if size & (size - 1):
            return lax.psum(flat, axes)
        bit = 1
        while bit < size:
            stages.append((axis, bit))
            bit *= 2
    if flat.shape[0] % (1 << len(stages)):
        return lax.psum(flat, axes)
    buf = flat
    for axis, bit in stages:
        half = buf.shape[0] // 2
        high = (lax.axis_index(axis) & bit) != 0
        low_part, high_part = buf[:half], buf[half:]
        send = jnp.where(high, low_part, high_part)
        keep = jnp.where(high, high_part, low_part)
        buf = keep + xor_swap(send, axis, bit)
    for axis, bit in reversed(stages):
        high = (lax.axis_index(axis) & bit) != 0
        other = xor_swap(buf, axis, bit)
        buf = jnp.where(high, jnp.concatenate([other, buf]), jnp.concatenate([buf, other]))
    return buf


def gelu_tanh(value):
    return jax.nn.gelu(value, approximate=True)


def shards(
    inputs,
    cotangent,
    weight_first,
    weight_second,
    slot_tile,
    neighbour_tile,
    neighbour_turns,
    corner_live,
):
    count = slot_tile.shape[0]
    devices = lax.axis_size("space")
    me = lax.axis_index("space")
    offs = residues(devices)
    slot_of_tile = (
        jnp.zeros((count,), jnp.int32).at[slot_tile].set(jnp.arange(count, dtype=jnp.int32))
    )
    tables = (slot_tile, slot_of_tile, neighbour_tile, neighbour_turns, corner_live)
    plan = make_plan(me, tables, devices, offs)
    tile = inputs[0]
    cot_tile = cotangent[0]
    samples_all = tile.shape[0] * lax.axis_size("dp") * devices
    scale = 1.0 / math.sqrt(samples_all * tile.shape[1] * tile.shape[2])

    got_in = exchange(edge_rims(tile), offs)
    full_second = conv_full(cot_tile, weight_second)
    back_second = return_rims(send_buffers(full_second, plan, offs), offs)

    padded_in = pad_tile(tile, got_in, plan)
    hidden = conv_valid(padded_in, weight_first)
    active = gelu_tanh(hidden).astype(jnp.bfloat16)
    got_act = exchange(edge_rims(active), offs)
    padded_act = pad_tile(active, got_act, plan)
    local_second = weight_grad(padded_act, cot_tile)

    grad_active = add_rims(full_second[:, 1:-1, 1:-1], back_second)
    _, pull_gelu = jax.vjp(gelu_tanh, hidden)
    grad_hidden = pull_gelu(grad_active)[0].astype(jnp.bfloat16)
    local_first = weight_grad(padded_in, grad_hidden)
    full_first = conv_full(grad_hidden, weight_first)
    back_first = return_rims(send_buffers(full_first, plan, offs), offs)
    grad_tile = add_rims(full_first[:, 1:-1, 1:-1], back_first).astype(jnp.bfloat16)

    flat = jnp.concatenate([local_first.reshape(-1), local_second.reshape(-1)])
    summed = all_reduce(flat, ("dp", "space"))
    half = local_first.size
    summed_first = summed[:half].reshape(local_first.shape)
    summed_second = summed[half:].reshape(local_second.shape)
    return (grad_tile[None], summed_first * scale, summed_second * scale)


def solution(mesh):
    in_specs = (
        P("space", "dp", None, None, None),
        P("space", "dp", None, None, None),
        P(),
        P(),
        P(),
        P(),
        P(),
        P(),
    )
    out_specs = (P("space", "dp", None, None, None), P(), P())
    return jax.shard_map(shards, mesh=mesh, in_specs=in_specs, out_specs=out_specs, check_vma=False)
```

profile of v0, /device:TPU:0, one launch (start us, length us, event | category | flops | bytes accessed | tf_op | source)
XLA Modules:
  0.0 362.0 jit_solution(15528731652978195346)
XLA Ops:
  3.1 6.0 %collective-permute-start.7 = (bf16[4,1,48,128]{3,2,0,1:T(8,128)(2,1)}, bf16[4,1,48,128]{3,2,0,1:T(8,128)(2,1)}, u32[]{:S(2)}, u32[]{:S(2)}) collective-permute-start(bf16[4,1,48,128]{3,2,0,1:T(8,128)(2,1)} %get-tuple-element.170), channel_id=1, source_target_pairs={{0,7},{1,0},{2,1},{3,2},{4,3},{5,4},{6,5},{7,6},{8,15},{9,8},{10,9... | collective-permute-start | bytes 147464 | tf_op jit(solution)/shard_map/ppermute | solution.py:42
  9.5 3.0 collective-permute-start.10
  18.5 1.8 convolution_select_fusion.1
  73.8 2.5 fusion.234
  109.3 1.7 copy.178
  121.1 1.9 collective-permute-start.12
  123.0 1.4 bitcast_dynamic-update-slice_fusion.14
  125.6 1.4 bitcast_dynamic-update-slice_fusion.13
  127.0 1.9 collective-permute-start
  128.9 1.4 bitcast_dynamic-update-slice_fusion.12
  130.4 2.5 collective-permute-start.1
  132.8 1.4 bitcast_dynamic-update-slice_fusion.11
  134.3 1.4 bitcast_dynamic-update-slice_fusion.10
  135.7 2.9 collective-permute-start.3
  139.8 1.5 dynamic-slice_bitcast_fusion.15
  165.8 2.1 reshape.2221
  169.3 4.6 %multiply_convert_fusion = (bf16[48,8,7,128]{3,1,2,0:T(8,128)(2,1)S(1)}, f32[48,8,7,128]{3,1,2,0:T(8,128)}, f32[48,8,7,128]{3,1,2,0:T(8,128)}, f32[48,8,7,128]{3,1,2,0:T(8,128)}, f32[48,8,7,128]{3,1,2,0:T(8,128)}) fusion(bf16[3,3,128,128]{3,2,1,0:T(8,128)(2,1)S(1)} %copy-done, bf16[50,1,7,2,128]{4,2,3,0,1:T(8,128)(2,1)S(1)} %slice.921, ...), kind=kOutput, calls=%fused_computation.21 | convolution fusion | flops 799961088 | bytes 7384120 | tf_op jit(solution)/shard_map/conv_general_dilated | solution.py:95
  176.0 1.6 maximum_maximum_fusion.1
  179.4 1.3 reshape.2227
  183.4 1.3 reshape.2229
  186.2 2.4 collective-permute-start.21
  189.3 2.8 copy.131
  192.1 1.4 copy.132
  193.8 1.4 copy.133
  197.2 3.6 %collective-permute-done.22 = bf16[4,1,48,128]{3,2,0,1:T(8,128)(2,1)S(1)} collective-permute-done((bf16[4,1,48,128]{3,2,0,1:T(8,128)(2,1)S(1)}, bf16[4,1,48,128]{3,2,0,1:T(8,128)(2,1)S(1)}, u32[]{:S(2)}, u32[]{:S(2)}) %collective-permute-start.22) | collective-permute-done | bytes 49184 | tf_op jit(solution)/shard_map/ppermute | solution.py:42
  200.9 5.0 %collective-permute-done.23 = bf16[4,1,48,128]{3,2,0,1:T(8,128)(2,1)S(1)} collective-permute-done((bf16[4,1,48,128]{3,2,0,1:T(8,128)(2,1)S(1)}, bf16[4,1,48,128]{3,2,0,1:T(8,128)(2,1)S(1)}, u32[]{:S(2)}, u32[]{:S(2)}) %collective-permute-start.23) | collective-permute-done | bytes 49184 | tf_op jit(solution)/shard_map/ppermute | solution.py:42
  206.1 4.7 %collective-permute-done.24 = bf16[4,1,48,128]{3,2,0,1:T(8,128)(2,1)S(1)} collective-permute-done((bf16[4,1,48,128]{3,2,0,1:T(8,128)(2,1)S(1)}, bf16[4,1,48,128]{3,2,0,1:T(8,128)(2,1)S(1)}, u32[]{:S(2)}, u32[]{:S(2)}) %collective-permute-start.24) | collective-permute-done | bytes 49184 | tf_op jit(solution)/shard_map/ppermute | solution.py:42
  210.8 1.7 collective-permute-start.25
  212.6 4.2 %collective-permute-done.25 = bf16[4,1,48,128]{3,2,0,1:T(8,128)(2,1)S(1)} collective-permute-done((bf16[4,1,48,128]{3,2,0,1:T(8,128)(2,1)S(1)}, bf16[4,1,48,128]{3,2,0,1:T(8,128)(2,1)S(1)}, u32[]{:S(2)}, u32[]{:S(2)}) %collective-permute-start.25) | collective-permute-done | bytes 49184 | tf_op jit(solution)/shard_map/ppermute | solution.py:42
  216.7 2.2 collective-permute-start.26
  218.9 4.4 %collective-permute-done.26 = bf16[4,1,48,128]{3,2,0,1:T(8,128)(2,1)S(1)} collective-permute-done((bf16[4,1,48,128]{3,2,0,1:T(8,128)(2,1)S(1)}, bf16[4,1,48,128]{3,2,0,1:T(8,128)(2,1)S(1)}, u32[]{:S(2)}, u32[]{:S(2)}) %collective-permute-start.26) | collective-permute-done | bytes 49184 | tf_op jit(solution)/shard_map/ppermute | solution.py:42
  223.3 2.5 collective-permute-start.27
  225.8 4.3 %collective-permute-done.27 = bf16[4,1,48,128]{3,2,1,0:T(8,128)(2,1)S(1)} collective-permute-done((bf16[4,1,48,128]{3,2,1,0:T(8,128)(2,1)S(1)}, bf16[4,1,48,128]{3,2,1,0:T(8,128)(2,1)S(1)}, u32[]{:S(2)}, u32[]{:S(2)}) %collective-permute-start.27) | collective-permute-done | bytes 49184 | tf_op jit(solution)/shard_map/ppermute | solution.py:42
  232.1 1.8 fusion.214
  233.9 1.3 rev.97
  237.9 1.8 fusion.216
  241.0 1.8 fusion.210
  246.8 1.8 fusion.212
  254.8 2.0 maximum_maximum_fusion
  264.6 2.4 collective-permute-start.6
  274.0 2.8 fusion.9
  284.7 1.8 convolution_select_fusion
  287.9 3.1 fusion.230
  292.1 1.3 rev.87
  293.5 1.3 rev.88
  300.7 1.6 collective-permute-start.29
  302.7 7.6 %collective-permute-done.29 = f32[73728]{0:T(1024)S(1)} collective-permute-done((f32[73728]{0:T(1024)S(1)}, f32[73728]{0:T(1024)S(1)}, u32[]{:S(2)}, u32[]{:S(2)}) %collective-permute-start.29) | collective-permute-done | bytes 294944 | tf_op jit(solution)/shard_map/ppermute | solution.py:171
  310.3 1.7 collective-permute-start.30
  312.2 3.6 %collective-permute-done.30 = f32[36864]{0:T(1024)S(1)} collective-permute-done((f32[36864]{0:T(1024)S(1)}, f32[36864]{0:T(1024)S(1)}, u32[]{:S(2)}, u32[]{:S(2)}) %collective-permute-start.30) | collective-permute-done | bytes 147488 | tf_op jit(solution)/shard_map/ppermute | solution.py:171
  315.9 1.9 collective-permute-start.31
  318.0 2.3 collective-permute-done.31
  320.3 2.8 collective-permute-start.32
  323.3 2.0 collective-permute-done.32
  325.3 2.8 collective-permute-start.33
  328.2 1.8 collective-permute-start.14
  330.0 2.5 collective-permute-start.15
  332.8 1.6 collective-permute-start.16
  334.4 3.8 %collective-permute-start.17 = (f32[4,1,48,128]{3,2,1,0:T(8,128)S(1)}, f32[4,1,48,128]{3,2,1,0:T(8,128)S(1)}, u32[]{:S(2)}, u32[]{:S(2)}) collective-permute-start(f32[4,1,48,128]{3,2,1,0:T(8,128)S(1)} %fusion.174), channel_id=1, source_target_pairs={{0,4},{1,5},{2,6},{3,7},{4,0},{5,1},{6,2},{7,3},{8,12},{9,13},{10,... | collective-permute-start | bytes 294920 | tf_op jit(solution)/shard_map/ppermute | solution.py:42
  339.7 1.9 collective-permute-start.19
  341.7 4.9 %collective-permute-start.20 = (f32[4,1,48,128]{3,2,1,0:T(8,128)S(1)}, f32[4,1,48,128]{3,2,1,0:T(8,128)S(1)}, u32[]{:S(2)}, u32[]{:S(2)}) collective-permute-start(f32[4,1,48,128]{3,2,1,0:T(8,128)S(1)} %fusion.195), channel_id=1, source_target_pairs={{0,7},{1,0},{2,1},{3,2},{4,3},{5,4},{6,5},{7,6},{8,15},{9,8},{10,9... | collective-permute-start | bytes 294920 | tf_op jit(solution)/shard_map/ppermute | solution.py:42
  346.7 2.1 collective-permute-done.20
  349.0 2.8 collective-permute-done.35
  351.8 1.6 collective-permute-start.36
  353.7 4.9 %collective-permute-done.36 = f32[73728]{0:T(1024)S(1)} collective-permute-done((f32[73728]{0:T(1024)S(1)}, f32[73728]{0:T(1024)S(1)}, u32[]{:S(2)}, u32[]{:S(2)}) %collective-permute-start.36) | collective-permute-done | bytes 294944 | tf_op jit(solution)/shard_map/ppermute | solution.py:171
  (413 shorter events, 121.3 us)
Async XLA Ops:
  0.6 168.6 %copy-start = (bf16[3,3,128,128]{3,2,1,0:T(8,128)(2,1)S(1)}, bf16[3,3,128,128]{3,2,1,0:T(8,128)(2,1)}, u32[]{:S(2)}) copy-start(bf16[3,3,128,128]{3,2,1,0:T(8,128)(2,1)} %param.30) | copy-start | bytes 884740
  3.1 118.1 %collective-permute-start.7 = (bf16[4,1,48,128]{3,2,0,1:T(8,128)(2,1)}, bf16[4,1,48,128]{3,2,0,1:T(8,128)(2,1)}, u32[]{:S(2)}, u32[]{:S(2)}) collective-permute-start(bf16[4,1,48,128]{3,2,0,1:T(8,128)(2,1)} %get-tuple-element.170), channel_id=1, source_target_pairs={{0,7},{1,0},{2,1},{3,2},{4,3},{5,4},{6,5},{7,6},{8,15},{9,8},{10,9... | collective-permute-start | bytes 147464 | tf_op jit(solution)/shard_map/ppermute | solution.py:42
  9.1 115.4 %collective-permute-start.8 = (bf16[4,1,48,128]{3,2,0,1:T(8,128)(2,1)}, bf16[4,1,48,128]{3,2,0,1:T(8,128)(2,1)}, u32[]{:S(2)}, u32[]{:S(2)}) collective-permute-start(bf16[4,1,48,128]{3,2,0,1:T(8,128)(2,1)} %get-tuple-element.170), channel_id=1, source_target_pairs={{0,6},{1,7},{2,0},{3,1},{4,2},{5,3},{6,4},{7,5},{8,14},{9,15},{10,... | collective-permute-start | bytes 147464 | tf_op jit(solution)/shard_map/ppermute | solution.py:42
  9.5 117.5 %collective-permute-start.9 = (bf16[4,1,48,128]{3,2,0,1:T(8,128)(2,1)}, bf16[4,1,48,128]{3,2,0,1:T(8,128)(2,1)}, u32[]{:S(2)}, u32[]{:S(2)}) collective-permute-start(bf16[4,1,48,128]{3,2,0,1:T(8,128)(2,1)} %get-tuple-element.170), channel_id=1, source_target_pairs={{0,5},{1,6},{2,7},{3,0},{4,1},{5,2},{6,3},{7,4},{8,13},{9,14},{10,... | collective-permute-start | bytes 147464 | tf_op jit(solution)/shard_map/ppermute | solution.py:42
  9.5 120.8 %collective-permute-start.10 = (bf16[4,1,48,128]{3,2,0,1:T(8,128)(2,1)}, bf16[4,1,48,128]{3,2,0,1:T(8,128)(2,1)}, u32[]{:S(2)}, u32[]{:S(2)}) collective-permute-start(bf16[4,1,48,128]{3,2,0,1:T(8,128)(2,1)} %get-tuple-element.170), channel_id=1, source_target_pairs={{0,4},{1,5},{2,6},{3,7},{4,0},{5,1},{6,2},{7,3},{8,12},{9,13},{10,... | collective-permute-start | bytes 147464 | tf_op jit(solution)/shard_map/ppermute | solution.py:42
  12.5 121.8 %collective-permute-start.11 = (bf16[4,1,48,128]{3,2,0,1:T(8,128)(2,1)}, bf16[4,1,48,128]{3,2,0,1:T(8,128)(2,1)}, u32[]{:S(2)}, u32[]{:S(2)}) collective-permute-start(bf16[4,1,48,128]{3,2,0,1:T(8,128)(2,1)} %get-tuple-element.170), channel_id=1, source_target_pairs={{0,3},{1,4},{2,5},{3,6},{4,7},{5,0},{6,1},{7,2},{8,11},{9,12},{10,... | collective-permute-start | bytes 147464 | tf_op jit(solution)/shard_map/ppermute | solution.py:42
  21.0 39.1 %copy-start.2 = (s32[4,4]{1,0:T(4,128)S(1)}, s32[4,4]{1,0:T(4,128)}, u32[]{:S(2)}) copy-start(s32[4,4]{1,0:T(4,128)} %constant.333.clone) | copy-start | bytes 196
  21.0 40.4 %copy-start.1 = (s32[4,4]{1,0:T(4,128)S(1)}, s32[4,4]{1,0:T(4,128)}, u32[]{:S(2)}) copy-start(s32[4,4]{1,0:T(4,128)} %constant.334.clone) | copy-start | bytes 196
  21.0 42.4 %copy-start.75 = (s32[8,4]{0,1:T(4,128)S(1)}, s32[8,4]{0,1:T(4,128)}, u32[]{:S(2)}) copy-start(s32[8,4]{0,1:T(4,128)} %param.35) | copy-start | bytes 388
  68.4 8.0 %copy-start.72 = (pred[48]{0:T(512)(128)(4,1)}, pred[48]{0:T(512)(128)(4,1)S(1)}, u32[]{:S(2)}) copy-start(pred[48]{0:T(512)(128)(4,1)S(1)} %iota_compare_fusion.2) | copy-start | bytes 148
  68.5 8.2 %copy-start.73 = (pred[48]{0:T(512)(128)(4,1)}, pred[48]{0:T(512)(128)(4,1)S(1)}, u32[]{:S(2)}) copy-start(pred[48]{0:T(512)(128)(4,1)S(1)} %iota_compare_fusion.4) | copy-start | bytes 148
  68.5 8.2 %copy-start.74 = (pred[48]{0:T(512)(128)(4,1)}, pred[48]{0:T(512)(128)(4,1)S(1)}, u32[]{:S(2)}) copy-start(pred[48]{0:T(512)(128)(4,1)S(1)} %iota_compare_fusion.6) | copy-start | bytes 148
  68.5 8.1 %copy-start.71 = (pred[48]{0:T(512)(128)(4,1)}, pred[48]{0:T(512)(128)(4,1)S(1)}, u32[]{:S(2)}) copy-start(pred[48]{0:T(512)(128)(4,1)S(1)} %iota_compare_fusion.8) | copy-start | bytes 148
  70.6 198.6 %copy-start.36 = (pred[4]{0:T(512)(128)(4,1)}, pred[4]{0:T(512)(128)(4,1)S(1)}, u32[]{:S(2)}) copy-start(pred[4]{0:T(512)(128)(4,1)S(1)} %iota_compare_fusion.12) | copy-start | bytes 16
  71.3 197.9 %copy-start.38 = (pred[4]{0:T(512)(128)(4,1)}, pred[4]{0:T(512)(128)(4,1)S(1)}, u32[]{:S(2)}) copy-start(pred[4]{0:T(512)(128)(4,1)S(1)} %iota_compare_fusion.13) | copy-start | bytes 16
  71.9 197.3 %copy-start.40 = (pred[4]{0:T(512)(128)(4,1)}, pred[4]{0:T(512)(128)(4,1)S(1)}, u32[]{:S(2)}) copy-start(pred[4]{0:T(512)(128)(4,1)S(1)} %iota_compare_fusion.3) | copy-start | bytes 16
  72.5 196.7 %copy-start.42 = (pred[4]{0:T(512)(128)(4,1)}, pred[4]{0:T(512)(128)(4,1)S(1)}, u32[]{:S(2)}) copy-start(pred[4]{0:T(512)(128)(4,1)S(1)} %iota_compare_fusion.5) | copy-start | bytes 16
  73.2 196.1 %copy-start.44 = (pred[4]{0:T(512)(128)(4,1)}, pred[4]{0:T(512)(128)(4,1)S(1)}, u32[]{:S(2)}) copy-start(pred[4]{0:T(512)(128)(4,1)S(1)} %iota_compare_fusion.7) | copy-start | bytes 16
  73.8 195.5 %copy-start.46 = (pred[4]{0:T(512)(128)(4,1)}, pred[4]{0:T(512)(128)(4,1)S(1)}, u32[]{:S(2)}) copy-start(pred[4]{0:T(512)(128)(4,1)S(1)} %iota_compare_fusion.9) | copy-start | bytes 16
  76.5 32.7 %copy-start.9 = (f32[48,128]{1,0:T(8,128)}, f32[48,128]{1,0:T(8,128)S(1)}, u32[]{:S(2)}) copy-start(f32[48,128]{1,0:T(8,128)S(1)} %broadcast_select_fusion.5) | copy-start | bytes 73732
  76.6 32.6 %copy-start.11 = (f32[48,128]{1,0:T(8,128)}, f32[48,128]{1,0:T(8,128)S(1)}, u32[]{:S(2)}) copy-start(f32[48,128]{1,0:T(8,128)S(1)} %broadcast_select_fusion.6) | copy-start | bytes 73732
  76.7 32.5 %copy-start.13 = (f32[48,128]{1,0:T(8,128)}, f32[48,128]{1,0:T(8,128)S(1)}, u32[]{:S(2)}) copy-start(f32[48,128]{1,0:T(8,128)S(1)} %broadcast_select_fusion.7) | copy-start | bytes 73732
  76.7 32.5 %copy-start.15 = (f32[48,128]{1,0:T(8,128)}, f32[48,128]{1,0:T(8,128)S(1)}, u32[]{:S(2)}) copy-start(f32[48,128]{1,0:T(8,128)S(1)} %select_bitcast_fusion.4) | copy-start | bytes 73732
  76.7 32.5 %copy-start.17 = (f32[48,128]{1,0:T(8,128)}, f32[48,128]{1,0:T(8,128)S(1)}, u32[]{:S(2)}) copy-start(f32[48,128]{1,0:T(8,128)S(1)} %select_bitcast_fusion.5) | copy-start | bytes 73732
  76.7 32.5 %copy-start.19 = (f32[48,128]{1,0:T(8,128)}, f32[48,128]{1,0:T(8,128)S(1)}, u32[]{:S(2)}) copy-start(f32[48,128]{1,0:T(8,128)S(1)} %get-tuple-element.119) | copy-start | bytes 73732
  76.7 32.5 %copy-start.21 = (f32[48,128]{1,0:T(8,128)}, f32[48,128]{1,0:T(8,128)S(1)}, u32[]{:S(2)}) copy-start(f32[48,128]{1,0:T(8,128)S(1)} %get-tuple-element.120) | copy-start | bytes 73732
  109.2 54.5 %copy-start.3 = (bf16[1,1,48,48,128]{4,3,2,1,0:T(8,128)(2,1)S(1)}, bf16[1,1,48,48,128]{4,3,2,1,0:T(8,128)(2,1)}, u32[]{:S(2)}) copy-start(bf16[1,1,48,48,128]{4,3,2,1,0:T(8,128)(2,1)} %param.28) | copy-start | bytes 1769476
  121.1 14.5 %collective-permute-start.12 = (bf16[4,1,48,128]{3,2,0,1:T(8,128)(2,1)}, bf16[4,1,48,128]{3,2,0,1:T(8,128)(2,1)S(1)}, u32[]{:S(2)}, u32[]{:S(2)}) collective-permute-start(bf16[4,1,48,128]{3,2,0,1:T(8,128)(2,1)} %get-tuple-element.170), channel_id=1, source_target_pairs={{0,2},{1,3},{2,4},{3,5},{4,6},{5,7},{6,0},{7,1},{8,10},{9,11},{10,... | collective-permute-start | bytes 147464 | tf_op jit(solution)/shard_map/ppermute | solution.py:42
  124.5 14.7 %collective-permute-start.13 = (bf16[4,1,48,128]{3,2,1,0:T(8,128)(2,1)}, bf16[4,1,48,128]{3,2,1,0:T(8,128)(2,1)S(1)}, u32[]{:S(2)}, u32[]{:S(2)}) collective-permute-start(bf16[4,1,48,128]{3,2,1,0:T(8,128)(2,1)} %get-tuple-element.169), channel_id=1, source_target_pairs={{0,1},{1,2},{2,3},{3,4},{4,5},{5,6},{6,7},{7,0},{8,9},{9,10},{10,1... | collective-permute-start | bytes 147464 | tf_op jit(solution)/shard_map/ppermute | solution.py:42
  127.0 136.9 %collective-permute-start = (f32[4,1,48,128]{3,2,1,0:T(8,128)}, f32[4,1,48,128]{3,2,1,0:T(8,128)}, u32[]{:S(2)}, u32[]{:S(2)}) collective-permute-start(f32[4,1,48,128]{3,2,1,0:T(8,128)} %fusion.90), channel_id=1, source_target_pairs={{0,1},{1,2},{2,3},{3,4},{4,5},{5,6},{6,7},{7,0},{8,9},{9,10},{10,1... | collective-permute-start | bytes 294920 | tf_op jit(solution)/shard_map/ppermute | solution.py:42
  130.4 134.2 %collective-permute-start.1 = (f32[4,1,48,128]{3,2,1,0:T(8,128)}, f32[4,1,48,128]{3,2,1,0:T(8,128)}, u32[]{:S(2)}, u32[]{:S(2)}) collective-permute-start(f32[4,1,48,128]{3,2,1,0:T(8,128)} %fusion.97), channel_id=1, source_target_pairs={{0,2},{1,3},{2,4},{3,5},{4,6},{5,7},{6,0},{7,1},{8,10},{9,11},{10,... | collective-permute-start | bytes 294920 | tf_op jit(solution)/shard_map/ppermute | solution.py:42
  134.3 133.8 %collective-permute-start.2 = (f32[4,1,48,128]{3,2,1,0:T(8,128)}, f32[4,1,48,128]{3,2,1,0:T(8,128)}, u32[]{:S(2)}, u32[]{:S(2)}) collective-permute-start(f32[4,1,48,128]{3,2,1,0:T(8,128)} %fusion.104), channel_id=1, source_target_pairs={{0,3},{1,4},{2,5},{3,6},{4,7},{5,0},{6,1},{7,2},{8,11},{9,12},{10,... | collective-permute-start | bytes 294920 | tf_op jit(solution)/shard_map/ppermute | solution.py:42
  135.7 132.4 %collective-permute-start.3 = (f32[4,1,48,128]{3,2,1,0:T(8,128)}, f32[4,1,48,128]{3,2,1,0:T(8,128)}, u32[]{:S(2)}, u32[]{:S(2)}) collective-permute-start(f32[4,1,48,128]{3,2,1,0:T(8,128)} %fusion.111), channel_id=1, source_target_pairs={{0,4},{1,5},{2,6},{3,7},{4,0},{5,1},{6,2},{7,3},{8,12},{9,13},{10,... | collective-permute-start | bytes 294920 | tf_op jit(solution)/shard_map/ppermute | solution.py:42
  186.2 10.6 %collective-permute-start.21 = (bf16[4,1,48,128]{3,2,0,1:T(8,128)(2,1)S(1)}, bf16[4,1,48,128]{3,2,0,1:T(8,128)(2,1)S(1)}, u32[]{:S(2)}, u32[]{:S(2)}) collective-permute-start(bf16[4,1,48,128]{3,2,0,1:T(8,128)(2,1)S(1)} %get-tuple-element.168), channel_id=1, source_target_pairs={{0,7},{1,0},{2,1},{3,2},{4,3},{5,4},{6,5},{7,6},{8,15},{9,8},{10,9... | collective-permute-start | bytes 147464 | tf_op jit(solution)/shard_map/ppermute | solution.py:42
  196.8 4.1 %collective-permute-start.22 = (bf16[4,1,48,128]{3,2,0,1:T(8,128)(2,1)S(1)}, bf16[4,1,48,128]{3,2,0,1:T(8,128)(2,1)S(1)}, u32[]{:S(2)}, u32[]{:S(2)}) collective-permute-start(bf16[4,1,48,128]{3,2,0,1:T(8,128)(2,1)S(1)} %get-tuple-element.168), channel_id=1, source_target_pairs={{0,6},{1,7},{2,0},{3,1},{4,2},{5,3},{6,4},{7,5},{8,14},{9,15},{10,... | collective-permute-start | bytes 147464 | tf_op jit(solution)/shard_map/ppermute | solution.py:42
  200.9 5.0 %collective-permute-start.23 = (bf16[4,1,48,128]{3,2,0,1:T(8,128)(2,1)S(1)}, bf16[4,1,48,128]{3,2,0,1:T(8,128)(2,1)S(1)}, u32[]{:S(2)}, u32[]{:S(2)}) collective-permute-start(bf16[4,1,48,128]{3,2,0,1:T(8,128)(2,1)S(1)} %get-tuple-element.168), channel_id=1, source_target_pairs={{0,5},{1,6},{2,7},{3,0},{4,1},{5,2},{6,3},{7,4},{8,13},{9,14},{10,... | collective-permute-start | bytes 147464 | tf_op jit(solution)/shard_map/ppermute | solution.py:42
  205.9 5.0 %collective-permute-start.24 = (bf16[4,1,48,128]{3,2,0,1:T(8,128)(2,1)S(1)}, bf16[4,1,48,128]{3,2,0,1:T(8,128)(2,1)S(1)}, u32[]{:S(2)}, u32[]{:S(2)}) collective-permute-start(bf16[4,1,48,128]{3,2,0,1:T(8,128)(2,1)S(1)} %get-tuple-element.168), channel_id=1, source_target_pairs={{0,4},{1,5},{2,6},{3,7},{4,0},{5,1},{6,2},{7,3},{8,12},{9,13},{10,... | collective-permute-start | bytes 147464 | tf_op jit(solution)/shard_map/ppermute | solution.py:42
  210.8 5.9 %collective-permute-start.25 = (bf16[4,1,48,128]{3,2,0,1:T(8,128)(2,1)S(1)}, bf16[4,1,48,128]{3,2,0,1:T(8,128)(2,1)S(1)}, u32[]{:S(2)}, u32[]{:S(2)}) collective-permute-start(bf16[4,1,48,128]{3,2,0,1:T(8,128)(2,1)S(1)} %get-tuple-element.168), channel_id=1, source_target_pairs={{0,3},{1,4},{2,5},{3,6},{4,7},{5,0},{6,1},{7,2},{8,11},{9,12},{10,... | collective-permute-start | bytes 147464 | tf_op jit(solution)/shard_map/ppermute | solution.py:42
  216.7 6.6 %collective-permute-start.26 = (bf16[4,1,48,128]{3,2,0,1:T(8,128)(2,1)S(1)}, bf16[4,1,48,128]{3,2,0,1:T(8,128)(2,1)S(1)}, u32[]{:S(2)}, u32[]{:S(2)}) collective-permute-start(bf16[4,1,48,128]{3,2,0,1:T(8,128)(2,1)S(1)} %get-tuple-element.168), channel_id=1, source_target_pairs={{0,2},{1,3},{2,4},{3,5},{4,6},{5,7},{6,0},{7,1},{8,10},{9,11},{10,... | collective-permute-start | bytes 147464 | tf_op jit(solution)/shard_map/ppermute | solution.py:42
  223.3 6.8 %collective-permute-start.27 = (bf16[4,1,48,128]{3,2,1,0:T(8,128)(2,1)S(1)}, bf16[4,1,48,128]{3,2,1,0:T(8,128)(2,1)S(1)}, u32[]{:S(2)}, u32[]{:S(2)}) collective-permute-start(bf16[4,1,48,128]{3,2,1,0:T(8,128)(2,1)S(1)} %get-tuple-element.167), channel_id=1, source_target_pairs={{0,1},{1,2},{2,3},{3,4},{4,5},{5,6},{6,7},{7,0},{8,9},{9,10},{10,1... | collective-permute-start | bytes 147464 | tf_op jit(solution)/shard_map/ppermute | solution.py:42
  230.1 37.9 %collective-permute-start.4 = (f32[4,1,48,128]{3,2,1,0:T(8,128)}, f32[4,1,48,128]{3,2,1,0:T(8,128)}, u32[]{:S(2)}, u32[]{:S(2)}) collective-permute-start(f32[4,1,48,128]{3,2,1,0:T(8,128)} %fusion.118), channel_id=1, source_target_pairs={{0,5},{1,6},{2,7},{3,0},{4,1},{5,2},{6,3},{7,4},{8,13},{9,14},{10,... | collective-permute-start | bytes 294920 | tf_op jit(solution)/shard_map/ppermute | solution.py:42
  263.9 5.5 %copy-start.18 = (f32[48,128]{1,0:T(8,128)S(1)}, f32[48,128]{1,0:T(8,128)}, u32[]{:S(2)}) copy-start(f32[48,128]{1,0:T(8,128)} %copy-done.17) | copy-start | bytes 73732
  263.9 4.7 %collective-permute-start.5 = (f32[4,1,48,128]{3,2,1,0:T(8,128)S(1)}, f32[4,1,48,128]{3,2,1,0:T(8,128)S(1)}, u32[]{:S(2)}, u32[]{:S(2)}) collective-permute-start(f32[4,1,48,128]{3,2,1,0:T(8,128)S(1)} %copy-done.55), channel_id=1, source_target_pairs={{0,6},{1,7},{2,0},{3,1},{4,2},{5,3},{6,4},{7,5},{8,14},{9,15},{10,... | collective-permute-start | bytes 294920 | tf_op jit(solution)/shard_map/ppermute | solution.py:42
  264.6 4.7 %collective-permute-start.6 = (f32[4,1,48,128]{3,2,1,0:T(8,128)S(1)}, f32[4,1,48,128]{3,2,1,0:T(8,128)S(1)}, u32[]{:S(2)}, u32[]{:S(2)}) collective-permute-start(f32[4,1,48,128]{3,2,1,0:T(8,128)S(1)} %copy-done.54), channel_id=1, source_target_pairs={{0,7},{1,0},{2,1},{3,2},{4,3},{5,4},{6,5},{7,6},{8,15},{9,8},{10,9... | collective-permute-start | bytes 294920 | tf_op jit(solution)/shard_map/ppermute | solution.py:42
  276.8 7.1 %copy-start.7 = (bf16[1,48,48,128]{3,1,2,0:T(8,128)(2,1)}, bf16[1,48,48,128]{3,1,2,0:T(8,128)(2,1)S(1)}, u32[]{:S(2)}) copy-start(bf16[1,48,48,128]{3,1,2,0:T(8,128)(2,1)S(1)} %fusion.9) | copy-start | bytes 1769476
  287.9 6.9 %copy-start.35 = (f32[1,48,1,128]{3,2,1,0:T(1,128)}, f32[1,48,1,128]{3,2,1,0:T(1,128)S(1)}, u32[]{:S(2)}) copy-start(f32[1,48,1,128]{3,2,1,0:T(1,128)S(1)} %get-tuple-element.113) | copy-start | bytes 73732
  292.1 8.6 %collective-permute-start.28 = (f32[147456]{0:T(1024)S(1)}, f32[147456]{0:T(1024)S(1)}, u32[]{:S(2)}, u32[]{:S(2)}) collective-permute-start(f32[147456]{0:T(1024)S(1)} %bitcast.552), channel_id=1, source_target_pairs={{0,8},{8,0},{16,24},{24,16},{1,9},{9,1},{17,25},{25,17},{2,10},{10... | collective-permute-start | bytes 1769480 | tf_op jit(solution)/shard_map/ppermute | solution.py:171
  300.7 9.5 %collective-permute-start.29 = (f32[73728]{0:T(1024)S(1)}, f32[73728]{0:T(1024)S(1)}, u32[]{:S(2)}, u32[]{:S(2)}) collective-permute-start(f32[73728]{0:T(1024)S(1)} %slice_select_fusion), channel_id=1, source_target_pairs={{0,16},{8,24},{16,0},{24,8},{1,17},{9,25},{17,1},{25,9},{2,18},{10... | collective-permute-start | bytes 884744 | tf_op jit(solution)/shard_map/ppermute | solution.py:171
  310.3 5.5 %collective-permute-start.30 = (f32[36864]{0:T(1024)S(1)}, f32[36864]{0:T(1024)S(1)}, u32[]{:S(2)}, u32[]{:S(2)}) collective-permute-start(f32[36864]{0:T(1024)S(1)} %slice_select_fusion.1), channel_id=1, source_target_pairs={{0,1},{1,0},{2,3},{3,2},{4,5},{5,4},{6,7},{7,6},{8,9},{9,8},{10,11... | collective-permute-start | bytes 442376 | tf_op jit(solution)/shard_map/ppermute | solution.py:171
  315.9 4.4 %collective-permute-start.31 = (f32[18432]{0:T(1024)S(1)}, f32[18432]{0:T(1024)S(1)}, u32[]{:S(2)}, u32[]{:S(2)}) collective-permute-start(f32[18432]{0:T(1024)S(1)} %slice_select_fusion.2), channel_id=1, source_target_pairs={{0,2},{1,3},{2,0},{3,1},{4,6},{5,7},{6,4},{7,5},{8,10},{9,11},{10,... | collective-permute-start | bytes 221192 | tf_op jit(solution)/shard_map/ppermute | solution.py:171
  320.3 4.9 %collective-permute-start.32 = (f32[9216]{0:T(1024)S(1)}, f32[9216]{0:T(1024)S(1)}, u32[]{:S(2)}, u32[]{:S(2)}) collective-permute-start(f32[9216]{0:T(1024)S(1)} %slice_select_fusion.3), channel_id=1, source_target_pairs={{0,4},{1,5},{2,6},{3,7},{4,0},{5,1},{6,2},{7,3},{8,12},{9,13},{10,... | collective-permute-start | bytes 110600 | tf_op jit(solution)/shard_map/ppermute | solution.py:171
  325.3 7.2 %collective-permute-start.33 = (f32[9216]{0:T(1024)S(1)}, f32[9216]{0:T(1024)S(1)}, u32[]{:S(2)}, u32[]{:S(2)}) collective-permute-start(f32[9216]{0:T(1024)S(1)} %select_add_fusion.3), channel_id=1, source_target_pairs={{0,4},{1,5},{2,6},{3,7},{4,0},{5,1},{6,2},{7,3},{8,12},{9,13},{10,... | collective-permute-start | bytes 110600 | tf_op jit(solution)/shard_map/ppermute | solution.py:171
  328.2 10.4 %collective-permute-start.14 = (f32[4,1,48,128]{3,2,1,0:T(8,128)S(1)}, f32[4,1,48,128]{3,2,1,0:T(8,128)S(1)}, u32[]{:S(2)}, u32[]{:S(2)}) collective-permute-start(f32[4,1,48,128]{3,2,1,0:T(8,128)S(1)} %fusion.153), channel_id=1, source_target_pairs={{0,1},{1,2},{2,3},{3,4},{4,5},{5,6},{6,7},{7,0},{8,9},{9,10},{10,1... | collective-permute-start | bytes 294920 | tf_op jit(solution)/shard_map/ppermute | solution.py:42
  330.0 9.7 %collective-permute-start.15 = (f32[4,1,48,128]{3,2,1,0:T(8,128)S(1)}, f32[4,1,48,128]{3,2,1,0:T(8,128)S(1)}, u32[]{:S(2)}, u32[]{:S(2)}) collective-permute-start(f32[4,1,48,128]{3,2,1,0:T(8,128)S(1)} %fusion.160), channel_id=1, source_target_pairs={{0,2},{1,3},{2,4},{3,5},{4,6},{5,7},{6,0},{7,1},{8,10},{9,11},{10,... | collective-permute-start | bytes 294920 | tf_op jit(solution)/shard_map/ppermute | solution.py:42
  332.5 9.2 %collective-permute-start.34 = (f32[18432]{0:T(1024)S(1)}, f32[18432]{0:T(1024)S(1)}, u32[]{:S(2)}, u32[]{:S(2)}) collective-permute-start(f32[18432]{0:T(1024)S(1)} %maximum_select_fusion.4), channel_id=1, source_target_pairs={{0,2},{1,3},{2,0},{3,1},{4,6},{5,7},{6,4},{7,5},{8,10},{9,11},{10,... | collective-permute-start | bytes 221192 | tf_op jit(solution)/shard_map/ppermute | solution.py:171
  332.8 13.8 %collective-permute-start.16 = (f32[4,1,48,128]{3,2,1,0:T(8,128)S(1)}, f32[4,1,48,128]{3,2,1,0:T(8,128)S(1)}, u32[]{:S(2)}, u32[]{:S(2)}) collective-permute-start(f32[4,1,48,128]{3,2,1,0:T(8,128)S(1)} %fusion.167), channel_id=1, source_target_pairs={{0,3},{1,4},{2,5},{3,6},{4,7},{5,0},{6,1},{7,2},{8,11},{9,12},{10,... | collective-permute-start | bytes 294920 | tf_op jit(solution)/shard_map/ppermute | solution.py:42
  334.4 12.3 %collective-permute-start.17 = (f32[4,1,48,128]{3,2,1,0:T(8,128)S(1)}, f32[4,1,48,128]{3,2,1,0:T(8,128)S(1)}, u32[]{:S(2)}, u32[]{:S(2)}) collective-permute-start(f32[4,1,48,128]{3,2,1,0:T(8,128)S(1)} %fusion.174), channel_id=1, source_target_pairs={{0,4},{1,5},{2,6},{3,7},{4,0},{5,1},{6,2},{7,3},{8,12},{9,13},{10,... | collective-permute-start | bytes 294920 | tf_op jit(solution)/shard_map/ppermute | solution.py:42
  338.6 14.8 %copy-start.53 = (f32[1,1,48,128]{3,2,1,0:T(8,128)S(1)}, f32[1,1,48,128]{3,2,1,0:T(8,128)}, u32[]{:S(2)}) copy-start(f32[1,1,48,128]{3,2,1,0:T(8,128)} %get-tuple-element.111) | copy-start | bytes 73732
  338.6 8.1 %collective-permute-start.18 = (f32[4,1,48,128]{3,2,1,0:T(8,128)S(1)}, f32[4,1,48,128]{3,2,1,0:T(8,128)S(1)}, u32[]{:S(2)}, u32[]{:S(2)}) collective-permute-start(f32[4,1,48,128]{3,2,1,0:T(8,128)S(1)} %fusion.181), channel_id=1, source_target_pairs={{0,5},{1,6},{2,7},{3,0},{4,1},{5,2},{6,3},{7,4},{8,13},{9,14},{10,... | collective-permute-start | bytes 294920 | tf_op jit(solution)/shard_map/ppermute | solution.py:42
  339.7 7.0 %collective-permute-start.19 = (f32[4,1,48,128]{3,2,1,0:T(8,128)S(1)}, f32[4,1,48,128]{3,2,1,0:T(8,128)S(1)}, u32[]{:S(2)}, u32[]{:S(2)}) collective-permute-start(f32[4,1,48,128]{3,2,1,0:T(8,128)S(1)} %fusion.188), channel_id=1, source_target_pairs={{0,6},{1,7},{2,0},{3,1},{4,2},{5,3},{6,4},{7,5},{8,14},{9,15},{10,... | collective-permute-start | bytes 294920 | tf_op jit(solution)/shard_map/ppermute | solution.py:42
  341.7 7.1 %collective-permute-start.20 = (f32[4,1,48,128]{3,2,1,0:T(8,128)S(1)}, f32[4,1,48,128]{3,2,1,0:T(8,128)S(1)}, u32[]{:S(2)}, u32[]{:S(2)}) collective-permute-start(f32[4,1,48,128]{3,2,1,0:T(8,128)S(1)} %fusion.195), channel_id=1, source_target_pairs={{0,7},{1,0},{2,1},{3,2},{4,3},{5,4},{6,5},{7,6},{8,15},{9,8},{10,9... | collective-permute-start | bytes 294920 | tf_op jit(solution)/shard_map/ppermute | solution.py:42
  346.6 5.2 %collective-permute-start.35 = (f32[36864]{0:T(1024)S(1)}, f32[36864]{0:T(1024)S(1)}, u32[]{:S(2)}, u32[]{:S(2)}) collective-permute-start(f32[36864]{0:T(1024)S(1)} %maximum_select_fusion.3), channel_id=1, source_target_pairs={{0,1},{1,0},{2,3},{3,2},{4,5},{5,4},{6,7},{7,6},{8,9},{9,8},{10,11... | collective-permute-start | bytes 442376 | tf_op jit(solution)/shard_map/ppermute | solution.py:171
  351.8 6.8 %collective-permute-start.36 = (f32[73728]{0:T(1024)S(1)}, f32[73728]{0:T(1024)S(1)}, u32[]{:S(2)}, u32[]{:S(2)}) collective-permute-start(f32[73728]{0:T(1024)S(1)} %maximum_select_fusion.2), channel_id=1, source_target_pairs={{0,16},{8,24},{16,0},{24,8},{1,17},{9,25},{17,1},{25,9},{2,18},{10... | collective-permute-start | bytes 884744 | tf_op jit(solution)/shard_map/ppermute | solution.py:171
  358.7 2.1 collective-permute-start.37
  (55 other events, 148.5 us)
where the time goes:
time: 365 us; the launch traced here: 362 us
  between operations  78.9 us (22%)
  local copies, waits for them, and re-layouts  78.6 us (22%)
  other arithmetic  63.6 us (17%)
  starting transfers between devices  62.5 us (17%)
  waiting for transfers between devices  53.7 us (15%)
  matrix products  24.6 us (7%)
    ppermute x28, starting transfers between devices, shift(): lax.ppermute(value, 'space', [(i, (i + by) % length) for i in range(lengt...  49.9 us
    ppermute x28, waiting for transfers between devices, shift(): lax.ppermute(value, 'space', [(i, (i + by) % length) for i in range(lengt...  29.5 us
    ppermute x10, waiting for transfers between devices, xor_swap(): return lax.ppermute(value, axis, [(i, i ^ bit) for i in range(size)])  24.2 us
    rev x16, local copies, waits for them, and re-layouts, pad_tile(): rows.append(jnp.where(flips[k] == 1, row[:, ::-1], row))  21 us
    dot_general x18, matrix products, weight_grad(): jnp.einsum('bijc,bijd->cd', window, cot, preferred_element_type=jnp.float32)  16.4 us
    unnamed x182, local copies, waits for them, and re-layouts  16 us
    ppermute x10, starting transfers between devices, xor_swap(): return lax.ppermute(value, axis, [(i, i ^ bit) for i in range(size)])  12.6 us
    convert_element_type x9, local copies, waits for them, and re-layouts, shards(): active = gelu_tanh(hidden).astype(jnp.bfloat16)  7.32 us
  transfers between devices with their start and end apart: 38, of which 16 were waited for; matrix products, arithmetic and copies ran while one was open for 38% of the time, Pallas kernels for 0%

commit v1 on v0

--- a/solution.py
+++ b/solution.py
@@ -53,15 +53,19 @@
     position = np.zeros((devices,), np.int32)
     for i, o in enumerate(offs):
         position[o] = i + 1
-    position = jnp.asarray(position)
-    from_idx = position[(owners - me) % devices]
-    to_res = (owners - me) % devices
+    res = (owners - me) % devices
+    src = jnp.asarray(position)[res]
     turns = neighbour_turns[tile_id]
     side_tab, flip_tab = side_tables()
-    need = jnp.asarray(np.array(NEED_SIDE, np.int32))
+    need = np.array(NEED_SIDE, np.int32)
     sides = jnp.asarray(side_tab)[turns, need]
     flips = jnp.asarray(flip_tab)[turns, need]
-    return from_idx, to_res, sides, flips, corner_live[tile_id]
+    return src, res, sides, flips, corner_live[tile_id]
+
+
+def flip_index(flips, size):
+    cells = jnp.arange(size, dtype=jnp.int32)[None, :]
+    return jnp.where(flips[:, None] == 1, size - 1 - cells, cells)
 
 
 def assemble(own, top, bottom, left, right, top_left, top_right, bottom_left, bottom_right):
@@ -72,23 +76,14 @@
 
 
 def pad_tile(tile, received, plan):
-    from_idx, to_res, sides, flips, live = plan
-    rows = []
-    for k in range(8):
-        row = received[from_idx[k], sides[k]]
-        rows.append(jnp.where(flips[k] == 1, row[:, ::-1], row))
-    flags = live.astype(tile.dtype)
-    return assemble(
-        tile,
-        rows[0],
-        rows[1],
-        rows[2],
-        rows[3],
-        rows[4][:, -1] * flags[0],
-        rows[5][:, 0] * flags[1],
-        rows[6][:, -1] * flags[2],
-        rows[7][:, 0] * flags[3],
-    )
+    src, res, sides, flips, live = plan
+    size = tile.shape[1]
+    cells = flip_index(flips, size)
+    picked = received[src[:, None], sides[:, None], :, cells]
+    rows = picked.transpose(0, 2, 1, 3)
+    corners = jnp.stack([rows[4][:, -1], rows[5][:, 0], rows[6][:, -1], rows[7][:, 0]])
+    corners = corners * live.astype(tile.dtype)[:, None, None]
+    return assemble(tile, rows[0], rows[1], rows[2], rows[3], corners[0], corners[1], corners[2], corners[3])
 
 
 def conv_valid(padded, weight):
@@ -115,49 +110,41 @@
 
 
 def weight_grad(padded, cot):
-    size = cot.shape[1]
-    taps = []
-    for di in range(3):
-        row = []
-        for dj in range(3):
-            window = padded[:, di : di + size, dj : dj + size]
-            row.append(jnp.einsum("bijc,bijd->cd", window, cot, preferred_element_type=jnp.float32))
-        taps.append(jnp.stack(row))
-    return jnp.stack(taps)
+    return lax.conv_general_dilated(
+        padded,
+        cot,
+        (1, 1),
+        "VALID",
+        dimension_numbers=("CHWN", "IHWO", "HWNC"),
+        preferred_element_type=jnp.float32,
+    )
 
 
 def send_buffers(full, plan, offs):
-    from_idx, to_res, sides, flips, live = plan
+    src, res, sides, flips, live = plan
     size = full.shape[1] - 2
-    flags = live.astype(jnp.float32)
-    rows = [full[:, 0, 1:-1], full[:, -1, 1:-1], full[:, 1:-1, 0], full[:, 1:-1, -1]]
-    corners = [full[:, 0, 0] * flags[0], full[:, 0, -1] * flags[1],
-               full[:, -1, 0] * flags[2], full[:, -1, -1] * flags[3]]
-    ends = (size - 1, 0, size - 1, 0)
-    cells = jnp.arange(size, dtype=jnp.int32)
-    placed = []
-    for k in range(8):
-        if k < 4:
-            vec = jnp.where(flips[k] == 1, rows[k][:, ::-1], rows[k])
-        else:
-            at = jnp.where(flips[k] == 1, size - 1 - ends[k - 4], ends[k - 4])
-            vec = jnp.where((cells == at)[None, :, None], corners[k - 4][:, None, :], 0.0)
-        pick = jnp.arange(4, dtype=jnp.int32) == sides[k]
-        placed.append(jnp.where(pick[:, None, None, None], vec[None], 0.0))
-    buffers = []
-    for res in [0] + list(offs):
-        total = None
-        for k in range(8):
-            term = jnp.where(to_res[k] == res, placed[k], 0.0)
-            total = term if total is None else total + term
-        buffers.append(total)
-    return buffers
+    rows = jnp.stack([full[:, 0, 1:-1], full[:, -1, 1:-1], full[:, 1:-1, 0], full[:, 1:-1, -1]])
+    values = jnp.stack([full[:, 0, 0], full[:, 0, -1], full[:, -1, 0], full[:, -1, -1]])
+    values = values * live.astype(jnp.float32)[:, None, None]
+    ends = np.zeros((4, size), np.float32)
+    ends[[0, 1, 2, 3], [size - 1, 0, size - 1, 0]] = 1.0
+    corner_rows = jnp.asarray(ends)[:, None, :, None] * values[:, :, None, :]
+    vecs = jnp.concatenate([rows, corner_rows]).transpose(0, 2, 1, 3)
+    vecs = vecs[jnp.arange(8)[:, None], flip_index(flips, size)]
+    targets = np.array([0] + list(offs), np.int32)
+    mask = (res[None, None, :] == targets[:, None, None]) & (
+        sides[None, None, :] == jnp.arange(4, dtype=jnp.int32)[None, :, None]
+    )
+    flat = vecs.reshape(8, -1)
+    buffers = jnp.sum(jnp.where(mask[..., None], flat[None, None], 0.0), axis=2)
+    shape = (len(targets), 4, size) + full.shape[:1] + full.shape[3:]
+    return buffers.reshape(shape).transpose(0, 1, 3, 2, 4)
 
 
 def return_rims(buffers, offs):
     total = buffers[0]
-    for o, buf in zip(offs, buffers[1:]):
-        total = total + shift(buf, o)
+    for i, o in enumerate(offs):
+        total = total + shift(buffers[i + 1], o)
     return total
 
 

time: 365 us -> 229 us (0.63)
  between operations: 78.9 us -> 4 us
  other arithmetic: 63.6 us -> 21.9 us
  waiting for transfers between devices: 53.7 us -> 35.9 us
    rev x24 -> x0, local copies, waits for them, and re-layouts: 25 us -> none  [the longest x16 21 us: pad_tile(): rows.append(jnp.where(flips[k] == 1, row[:, ::-1], row))]
    gather x1 -> x5, local copies, waits for them, and re-layouts: 0.64 us -> 20.1 us  [the longest x2 11.9 us: pad_tile(): picked = received[src[:, None], sides[:, None], :, cells]]
    mul x10 -> x4, other arithmetic: 18 us -> 0.3 us  [the longest x2 0.15 us: pad_tile(): corners = corners * live.astype(tile.dtype)[:, None, None]]
    ppermute x28, waiting for transfers between devices: 29.5 us -> 11.8 us  [shift(): lax.ppermute(value, 'space', [(i, (i + by) % length) for i in range(lengt...]
    dot_general x18 -> x0, matrix products: 16.4 us -> none  [weight_grad(): jnp.einsum('bijc,bijd->cd', window, cot, preferred_element_type=jnp.float32)]
    conv_general_dilated x0 -> x2, matrix products: none -> 15 us  [weight_grad(): lax.conv_general_dilated(padded, cot, (1, 1), 'VALID', dimension_numbers=...]
    squeeze x4 -> x19, local copies, waits for them, and re-layouts: 2.81 us -> 17.6 us  [the longest x14 14.3 us: return_rims(): total = total + shift(buffers[i + 1], o)]
    select_n x14 -> x2, other arithmetic: 8.52 us -> 0.03 us  [the longest x1 0.01 us: make_plan(): src = jnp.asarray(position)[res]]
where the time goes in v1:
time: 229 us; the launch traced here: 225 us
  local copies, waits for them, and re-layouts  75.7 us (33%)
  starting transfers between devices  64.6 us (28%)
  waiting for transfers between devices  35.9 us (16%)
  matrix products  22.8 us (10%)
  other arithmetic  21.9 us (10%)
  between operations  4 us (2%)
    ppermute x28, starting transfers between devices, shift(): lax.ppermute(value, 'space', [(i, (i + by) % length) for i in range(lengt...  55.9 us
    ppermute x10, waiting for transfers between devices, xor_swap(): return lax.ppermute(value, axis, [(i, i ^ bit) for i in range(size)])  24.1 us
    conv_general_dilated x2, matrix products, weight_grad(): lax.conv_general_dilated(padded, cot, (1, 1), 'VALID', dimension_numbers=...  15 us
    squeeze x14, local copies, waits for them, and re-layouts, return_rims(): total = total + shift(buffers[i + 1], o)  14.3 us
    unnamed x85, local copies, waits for them, and re-layouts  14 us
    gather x2, local copies, waits for them, and re-layouts, pad_tile(): picked = received[src[:, None], sides[:, None], :, cells]  11.9 us
    ppermute x28, waiting for transfers between devices, shift(): lax.ppermute(value, 'space', [(i, (i + by) % length) for i in range(lengt...  11.8 us
    ppermute x10, starting transfers between devices, xor_swap(): return lax.ppermute(value, axis, [(i, i ^ bit) for i in range(size)])  8.72 us
  transfers between devices with their start and end apart: 38, of which 16 were waited for; matrix products, arithmetic and copies ran while one was open for 38% of the time, Pallas kernels for 0%

profile of v1, /device:TPU:0, one launch (start us, length us, event | category | flops | bytes accessed | tf_op | source)
XLA Modules:
  0.0 225.0 jit_solution(10008601220107224622)
XLA Ops:
  2.4 3.1 %collective-permute-start.12 = (bf16[4,1,48,128]{3,2,0,1:T(8,128)(2,1)S(1)}, bf16[4,1,48,128]{3,2,0,1:T(8,128)(2,1)}, u32[]{:S(2)}, u32[]{:S(2)}) collective-permute-start(bf16[4,1,48,128]{3,2,0,1:T(8,128)(2,1)S(1)} %pad_maximum_fusion.3), channel_id=1, source_target_pairs={{0,2},{1,3},{2,4},{3,5},{4,6},{5,7},{6,0},{7,1},{8,10},{9,11},{10,... | collective-permute-start | bytes 147464 | tf_op jit(solution)/shard_map/ppermute | solution.py:42
  5.5 2.5 %collective-permute-start.11 = (bf16[4,1,48,128]{3,2,0,1:T(8,128)(2,1)S(1)}, bf16[4,1,48,128]{3,2,0,1:T(8,128)(2,1)}, u32[]{:S(2)}, u32[]{:S(2)}) collective-permute-start(bf16[4,1,48,128]{3,2,0,1:T(8,128)(2,1)S(1)} %pad_maximum_fusion.3), channel_id=1, source_target_pairs={{0,3},{1,4},{2,5},{3,6},{4,7},{5,0},{6,1},{7,2},{8,11},{9,12},{10,... | collective-permute-start | bytes 147464 | tf_op jit(solution)/shard_map/ppermute | solution.py:42
  8.0 1.2 collective-permute-start.10
  9.3 2.6 %collective-permute-start.9 = (bf16[4,1,48,128]{3,2,0,1:T(8,128)(2,1)S(1)}, bf16[4,1,48,128]{3,2,0,1:T(8,128)(2,1)}, u32[]{:S(2)}, u32[]{:S(2)}) collective-permute-start(bf16[4,1,48,128]{3,2,0,1:T(8,128)(2,1)S(1)} %pad_maximum_fusion.3), channel_id=1, source_target_pairs={{0,5},{1,6},{2,7},{3,0},{4,1},{5,2},{6,3},{7,4},{8,13},{9,14},{10,... | collective-permute-start | bytes 147464 | tf_op jit(solution)/shard_map/ppermute | solution.py:42
  11.9 1.4 collective-permute-start.7
  13.3 1.2 dynamic_slice.12
  16.5 1.2 copy.196
  18.7 1.8 convolution_select_fusion.1
  27.1 3.7 %gather_fusion.3 = f32[384,128]{1,0:T(8,128)S(1)} fusion(f32[8,48,128]{2,1,0:T(8,128)S(1)} %bitcast.308, s32[384]{0:T(512)S(1)} %reshape.1035), kind=kCustom, calls=%fused_computation.3 | custom fusion | bytes 396288 | tf_op jit(solution)/shard_map/gather | solution.py:133
  30.9 2.3 %select_reduce_fusion.1 = f32[8,4,6144]{2,1,0:T(4,128)S(1)} fusion(f32[8,6144]{1,0:T(8,128)S(1)} %broadcast_in_dim.180, pred[8,4,8]{2,1,0:T(4,128)(4,1)S(1)} %broadcast_and_fusion), kind=kLoop, calls=%fused_computation.10 | loop fusion | flops 2949120 | bytes 983296 | tf_op jit(solution)/shard_map/reduce_sum | solution.py:139
  34.9 3.0 %copy.131 = bf16[1,48,48,128]{3,0,2,1:T(2,128)(2,1)} copy(bf16[1,48,48,128]{3,2,1,0:T(8,128)(2,1)} %bitcast.329) | data formatting | bytes 1179648 | tf_op jit(solution)/shard_map/squeeze | solution.py:211
  38.0 1.7 squeeze.113
  39.6 1.7 squeeze.119
  41.3 1.7 squeeze.118
  43.0 1.7 squeeze.117
  44.6 1.7 squeeze.116
  46.3 1.7 squeeze.115
  48.9 1.4 collective-permute-start.8
  51.1 1.9 collective-permute-done.8
  55.5 3.7 %collective-permute-start.2 = (f32[4,1,48,128]{3,1,2,0:T(1,128)}, f32[4,1,48,128]{3,1,2,0:T(1,128)}, u32[]{:S(2)}, u32[]{:S(2)}) collective-permute-start(f32[4,1,48,128]{3,1,2,0:T(1,128)} %squeeze.115), channel_id=1, source_target_pairs={{0,3},{1,4},{2,5},{3,6},{4,7},{5,0},{6,1},{7,2},{8,11},{9,12},{10,... | collective-permute-start | bytes 294920 | tf_op jit(solution)/shard_map/ppermute | solution.py:42
  60.1 1.7 collective-permute-start.3
  62.5 1.4 collective-permute-start.4
  64.8 11.2 %collective-permute-start.5 = (f32[4,1,48,128]{3,1,2,0:T(1,128)}, f32[4,1,48,128]{3,1,2,0:T(1,128)}, u32[]{:S(2)}, u32[]{:S(2)}) collective-permute-start(f32[4,1,48,128]{3,1,2,0:T(1,128)} %squeeze.118), channel_id=1, source_target_pairs={{0,6},{1,7},{2,0},{3,1},{4,2},{5,3},{6,4},{7,5},{8,14},{9,15},{10,... | collective-permute-start | bytes 294920 | tf_op jit(solution)/shard_map/ppermute | solution.py:42
  76.0 6.0 %gather_fusion.5 = bf16[384,128]{1,0:T(8,128)(2,1)S(1)} fusion(bf16[8,4,48,128]{3,2,1,0:T(8,128)(2,1)S(1)} %bitcast.326, s32[384]{0:T(512)S(1)} %reshape.1051), kind=kCustom, calls=%fused_computation.5 | custom fusion | bytes 201216 | tf_op jit(solution)/shard_map/gather | solution.py:82
  82.2 4.6 %pad_maximum_fusion = bf16[1,50,50,128]{3,0,2,1:T(2,128)(2,1)S(1)} fusion(bf16[1,1,50,128]{3,0,2,1:T(2,128)(2,1)S(1)} %copy.134, bf16[1,48,1,128]{3,0,2,1:T(2,128)(2,1)S(1)} %copy.132, bf16[1,48,48,128]{3,0,2,1:T(2,128)(2,1)} %copy.131, bf16[1,48,1,128]{3,0,2,1:T(2,128)(2,1)S(1)} %copy.130, bf16[1,1,50,128]{3,0,2,1:T(2,128)(2,1)S(1)} %copy.133), kind=kLoop, calls=%fused_computation.30 | loop fusion | flops 1280000 | bytes 1280000 | tf_op jit(solution)/shard_map/concatenate | solution.py:75
  89.1 2.2 reshape.961
  91.2 1.3 copy.136
  92.6 4.2 %multiply_convert_fusion = (bf16[48,8,7,128]{3,1,2,0:T(8,128)(2,1)S(1)}, f32[48,8,7,128]{3,1,2,0:T(8,128)S(1)}, f32[48,8,7,128]{3,1,2,0:T(8,128)}, f32[48,8,7,128]{3,1,2,0:T(8,128)}, f32[48,8,7,128]{3,1,2,0:T(8,128)}) fusion(bf16[3,3,128,128]{3,2,1,0:T(8,128)(2,1)S(1)} %copy-done, bf16[50,1,7,2,128]{4,2,3,0,1:T(8,128)(2,1)S(1)} %slice.723, ...), kind=kOutput, calls=%fused_computation.27 | convolution fusion | flops 799961088 | bytes 7384120 | tf_op jit(solution)/shard_map/conv_general_dilated | solution.py:90
  97.1 1.9 copy.165
  99.0 1.3 copy.139
  100.5 2.8 %copy.137 = f32[48,8,7,128]{3,0,2,1:T(8,128)} copy(f32[48,8,7,128]{3,1,2,0:T(8,128)} %get-tuple-element.122) | data formatting | bytes 2752512 | tf_op jit(solution)/shard_map/jvp()/mul | solution.py:189
  103.3 1.3 copy.140
  105.0 1.4 copy.138
  106.4 1.5 collective-permute-start.6
  108.5 1.4 collective-permute-start.26
  109.9 2.1 collective-permute-start.25
  112.0 3.1 %collective-permute-start.24 = (bf16[4,1,48,128]{3,2,0,1:T(8,128)(2,1)S(1)}, bf16[4,1,48,128]{3,2,0,1:T(8,128)(2,1)}, u32[]{:S(2)}, u32[]{:S(2)}) collective-permute-start(bf16[4,1,48,128]{3,2,0,1:T(8,128)(2,1)S(1)} %pad_maximum_fusion.4), channel_id=1, source_target_pairs={{0,4},{1,5},{2,6},{3,7},{4,0},{5,1},{6,2},{7,3},{8,12},{9,13},{10,... | collective-permute-start | bytes 147464 | tf_op jit(solution)/shard_map/ppermute | solution.py:42
  115.2 2.4 %collective-permute-start.21 = (bf16[4,1,48,128]{3,2,0,1:T(8,128)(2,1)S(1)}, bf16[4,1,48,128]{3,2,0,1:T(8,128)(2,1)}, u32[]{:S(2)}, u32[]{:S(2)}) collective-permute-start(bf16[4,1,48,128]{3,2,0,1:T(8,128)(2,1)S(1)} %pad_maximum_fusion.4), channel_id=1, source_target_pairs={{0,7},{1,0},{2,1},{3,2},{4,3},{5,4},{6,5},{7,6},{8,15},{9,8},{10,9... | collective-permute-start | bytes 147464 | tf_op jit(solution)/shard_map/ppermute | solution.py:42
  119.0 1.4 collective-permute-done.21
  120.4 2.3 %collective-permute-start.22 = (bf16[4,1,48,128]{3,2,0,1:T(8,128)(2,1)S(1)}, bf16[4,1,48,128]{3,2,0,1:T(8,128)(2,1)S(1)}, u32[]{:S(2)}, u32[]{:S(2)}) collective-permute-start(bf16[4,1,48,128]{3,2,0,1:T(8,128)(2,1)S(1)} %pad_maximum_fusion.4), channel_id=1, source_target_pairs={{0,6},{1,7},{2,0},{3,1},{4,2},{5,3},{6,4},{7,5},{8,14},{9,15},{10,... | collective-permute-start | bytes 147464 | tf_op jit(solution)/shard_map/ppermute | solution.py:42
  124.5 2.5 %collective-permute-start.27 = (bf16[4,1,48,128]{3,2,0,1:T(8,128)(2,1)S(1)}, bf16[4,1,48,128]{3,2,0,1:T(8,128)(2,1)S(1)}, u32[]{:S(2)}, u32[]{:S(2)}) collective-permute-start(bf16[4,1,48,128]{3,2,0,1:T(8,128)(2,1)S(1)} %pad_maximum_fusion.4), channel_id=1, source_target_pairs={{0,1},{1,2},{2,3},{3,4},{4,5},{5,6},{6,7},{7,0},{8,9},{9,10},{10,1... | collective-permute-start | bytes 147464 | tf_op jit(solution)/shard_map/ppermute | solution.py:42
  130.2 2.2 collective-permute-done.27
  132.5 6.0 %gather_fusion.7 = bf16[384,128]{1,0:T(8,128)(2,1)S(1)} fusion(bf16[8,4,48,128]{3,2,1,0:T(8,128)(2,1)S(1)} %bitcast.325, s32[384]{0:T(512)S(1)} %reshape.1051), kind=kCustom, calls=%fused_computation.7 | custom fusion | bytes 201216 | tf_op jit(solution)/shard_map/gather | solution.py:82
  139.3 2.4 %fusion.10 = bf16[1,48,48,128]{3,1,2,0:T(8,128)(2,1)S(1)} fusion(f32[48,1,56,128]{3,0,2,1:T(8,128)} %bitcast.314, f32[1,48,48,128]{3,1,2,0:T(8,128)S(1)} %fusion.43, f32[48,1,56,128]{3,0,2,1:T(8,128)} %bitcast.313, f32[48,1,56,128]{3,0,2,1:T(8,128)S(1)} %bitcast.312, f32[48,1,56,128]{3,0,2,1:T(8,128)} %bitcast.315), kind=kLoop, calls=%fused_computation.36 | loop fusion | flops 2949120 | bytes 6488064 | tf_op jit(solution)/shard_map/convert_element_type | solution.py:229
  142.6 1.8 convolution_select_fusion
  144.7 1.2 slice_bitcast_fusion
  146.7 7.3 %fusion.7 = f32[3,3,128,128]{3,2,1,0:T(8,128)S(1)} fusion(bf16[1,1,50,128]{3,0,2,1:T(2,128)(2,1)S(1)} %copy.168, bf16[1,48,1,128]{3,0,2,1:T(2,128)(2,1)S(1)} %copy.166, bf16[1,48,48,128]{3,0,2,1:T(2,128)(2,1)S(1)} %copy-done.13, bf16[1,48,1,128]{3,0,2,1:T(2,128)(2,1)S(1)} %copy.164, bf16[1,1,50,128]{3,0,2,1:T(2,128)(2,1)S(1)} %copy.167, ...), kind=kOutput, calls=%fused_computation.32 | convolution fusion | flops 682677248 | bytes 1819648 | tf_op jit(solution)/shard_map/conv_general_dilated | solution.py:113
  154.0 7.7 %broadcast_select_fusion = (f32[3,3,128,128]{3,2,1,0:T(8,128)S(1)}, f32[3,3,128,128]{3,2,1,0:T(8,128)S(1)}) fusion(f32[3,3,128,128]{3,2,1,0:T(8,128)S(1)} %fusion.7, pred[]{:T(512)S(6)} %ne.54, bf16[1,50,50,128]{3,0,2,1:T(2,128)(2,1)S(1)} %copy-done.7, bf16[1,48,48,128]{3,1,2,0:T(8,128)(2,1)S(1)} %copy-done.10), kind=kOutput, calls=%fused_computation.76 | convolution fusion | flops 679772160 | bytes 2999297 | tf_op jit(solution)/shard_map/conv_general_dilated | solution.py:113
  161.8 1.9 collective-permute-done.28
  163.9 1.6 collective-permute-start.29
  165.5 7.5 %collective-permute-done.29 = f32[73728]{0:T(1024)S(1)} collective-permute-done((f32[73728]{0:T(1024)S(1)}, f32[73728]{0:T(1024)S(1)}, u32[]{:S(2)}, u32[]{:S(2)}) %collective-permute-start.29) | collective-permute-done | bytes 294944 | tf_op jit(solution)/shard_map/ppermute | solution.py:158
  173.2 5.0 %collective-permute-done.30 = f32[36864]{0:T(1024)S(1)} collective-permute-done((f32[36864]{0:T(1024)S(1)}, f32[36864]{0:T(1024)S(1)}, u32[]{:S(2)}, u32[]{:S(2)}) %collective-permute-start.30) | collective-permute-done | bytes 147488 | tf_op jit(solution)/shard_map/ppermute | solution.py:158
  178.5 3.7 %gather_fusion.6 = f32[384,128]{1,0:T(8,128)S(1)} fusion(f32[8,48,128]{2,1,0:T(8,128)S(1)} %bitcast.309, s32[384]{0:T(512)S(1)} %copy-done.4), kind=kCustom, calls=%fused_computation.6 | custom fusion | bytes 396288 | tf_op jit(solution)/shard_map/gather | solution.py:133
  182.8 2.0 collective-permute-start.32
  184.8 2.3 %select_reduce_fusion = f32[8,4,6144]{2,1,0:T(4,128)S(1)} fusion(f32[8,6144]{1,0:T(8,128)S(1)} %broadcast_in_dim.188, pred[8,4,8]{2,1,0:T(4,128)(4,1)S(1)} %copy-done.18), kind=kLoop, calls=%fused_computation.9 | loop fusion | flops 2949120 | bytes 983296 | tf_op jit(solution)/shard_map/reduce_sum | solution.py:139
  187.7 2.0 collective-permute-start.33
  192.5 2.7 %collective-permute-done.33 = f32[9216]{0:T(1024)S(1)} collective-permute-done((f32[9216]{0:T(1024)S(1)}, f32[9216]{0:T(1024)S(1)}, u32[]{:S(2)}, u32[]{:S(2)}) %collective-permute-start.33) | collective-permute-done | bytes 36896 | tf_op jit(solution)/shard_map/ppermute | solution.py:158
  198.1 1.2 collective-permute-start.17
  199.3 3.2 %collective-permute-start.18 = (f32[4,1,48,128]{3,1,2,0:T(1,128)S(1)}, f32[4,1,48,128]{3,1,2,0:T(1,128)S(1)}, u32[]{:S(2)}, u32[]{:S(2)}) collective-permute-start(f32[4,1,48,128]{3,1,2,0:T(1,128)S(1)} %squeeze.132), channel_id=1, source_target_pairs={{0,5},{1,6},{2,7},{3,0},{4,1},{5,2},{6,3},{7,4},{8,13},{9,14},{10,... | collective-permute-start | bytes 294920 | tf_op jit(solution)/shard_map/ppermute | solution.py:42
  202.9 1.9 collective-permute-start.20
  207.1 1.3 collective-permute-start.35
  208.6 3.8 %collective-permute-done.14 = f32[4,1,48,128]{3,1,2,0:T(1,128)S(1)} collective-permute-done((f32[4,1,48,128]{3,1,2,0:T(1,128)}, f32[4,1,48,128]{3,1,2,0:T(1,128)S(1)}, u32[]{:S(2)}, u32[]{:S(2)}) %collective-permute-start.14) | collective-permute-done | bytes 98336 | tf_op jit(solution)/shard_map/ppermute | solution.py:42
  213.5 1.6 collective-permute-start.36
  215.3 5.0 %collective-permute-done.36 = f32[73728]{0:T(1024)} collective-permute-done((f32[73728]{0:T(1024)S(1)}, f32[73728]{0:T(1024)}, u32[]{:S(2)}, u32[]{:S(2)}) %collective-permute-start.36) | collective-permute-done | bytes 294944 | tf_op jit(solution)/shard_map/ppermute | solution.py:158
  (261 shorter events, 46.3 us)
Async XLA Ops:
  0.6 91.9 %copy-start = (bf16[3,3,128,128]{3,2,1,0:T(8,128)(2,1)S(1)}, bf16[3,3,128,128]{3,2,1,0:T(8,128)(2,1)}, u32[]{:S(2)}) copy-start(bf16[3,3,128,128]{3,2,1,0:T(8,128)(2,1)} %param.36) | copy-start | bytes 884740
  2.4 60.1 %collective-permute-start.12 = (bf16[4,1,48,128]{3,2,0,1:T(8,128)(2,1)S(1)}, bf16[4,1,48,128]{3,2,0,1:T(8,128)(2,1)}, u32[]{:S(2)}, u32[]{:S(2)}) collective-permute-start(bf16[4,1,48,128]{3,2,0,1:T(8,128)(2,1)S(1)} %pad_maximum_fusion.3), channel_id=1, source_target_pairs={{0,2},{1,3},{2,4},{3,5},{4,6},{5,7},{6,0},{7,1},{8,10},{9,11},{10,... | collective-permute-start | bytes 147464 | tf_op jit(solution)/shard_map/ppermute | solution.py:42
  5.5 54.6 %collective-permute-start.11 = (bf16[4,1,48,128]{3,2,0,1:T(8,128)(2,1)S(1)}, bf16[4,1,48,128]{3,2,0,1:T(8,128)(2,1)}, u32[]{:S(2)}, u32[]{:S(2)}) collective-permute-start(bf16[4,1,48,128]{3,2,0,1:T(8,128)(2,1)S(1)} %pad_maximum_fusion.3), channel_id=1, source_target_pairs={{0,3},{1,4},{2,5},{3,6},{4,7},{5,0},{6,1},{7,2},{8,11},{9,12},{10,... | collective-permute-start | bytes 147464 | tf_op jit(solution)/shard_map/ppermute | solution.py:42
  8.0 47.5 %collective-permute-start.10 = (bf16[4,1,48,128]{3,2,0,1:T(8,128)(2,1)S(1)}, bf16[4,1,48,128]{3,2,0,1:T(8,128)(2,1)}, u32[]{:S(2)}, u32[]{:S(2)}) collective-permute-start(bf16[4,1,48,128]{3,2,0,1:T(8,128)(2,1)S(1)} %pad_maximum_fusion.3), channel_id=1, source_target_pairs={{0,4},{1,5},{2,6},{3,7},{4,0},{5,1},{6,2},{7,3},{8,12},{9,13},{10,... | collective-permute-start | bytes 147464 | tf_op jit(solution)/shard_map/ppermute | solution.py:42
  9.3 44.4 %collective-permute-start.9 = (bf16[4,1,48,128]{3,2,0,1:T(8,128)(2,1)S(1)}, bf16[4,1,48,128]{3,2,0,1:T(8,128)(2,1)}, u32[]{:S(2)}, u32[]{:S(2)}) collective-permute-start(bf16[4,1,48,128]{3,2,0,1:T(8,128)(2,1)S(1)} %pad_maximum_fusion.3), channel_id=1, source_target_pairs={{0,5},{1,6},{2,7},{3,0},{4,1},{5,2},{6,3},{7,4},{8,13},{9,14},{10,... | collective-permute-start | bytes 147464 | tf_op jit(solution)/shard_map/ppermute | solution.py:42
  11.9 37.0 %collective-permute-start.7 = (bf16[4,1,48,128]{3,2,0,1:T(8,128)(2,1)S(1)}, bf16[4,1,48,128]{3,2,0,1:T(8,128)(2,1)}, u32[]{:S(2)}, u32[]{:S(2)}) collective-permute-start(bf16[4,1,48,128]{3,2,0,1:T(8,128)(2,1)S(1)} %pad_maximum_fusion.3), channel_id=1, source_target_pairs={{0,7},{1,0},{2,1},{3,2},{4,3},{5,4},{6,5},{7,6},{8,15},{9,8},{10,9... | collective-permute-start | bytes 147464 | tf_op jit(solution)/shard_map/ppermute | solution.py:42
  17.8 1.0 copy-start.26
  20.9 1.6 copy-start.2
  20.9 2.2 copy-start.1
  20.9 2.9 %copy-start.21 = (s32[8,4]{0,1:T(4,128)S(1)}, s32[8,4]{0,1:T(4,128)}, u32[]{:S(2)}) copy-start(s32[8,4]{0,1:T(4,128)} %param.41) | copy-start | bytes 388
  21.0 5.9 %copy-start.19 = (f32[4,48]{1,0:T(4,128)S(1)}, f32[4,48]{1,0:T(4,128)}, u32[]{:S(2)}) copy-start(f32[4,48]{1,0:T(4,128)} %constant.263.clone) | copy-start | bytes 2308
  24.0 3.1 %copy-start.22 = (f32[4]{0:T(128)}, f32[4]{0:T(128)S(1)}, u32[]{:S(2)}) copy-start(f32[4]{0:T(128)S(1)} %convert_reduce_fusion) | copy-start | bytes 52
  26.8 4.0 %copy-start.3 = (s32[384]{0:T(512)}, s32[384]{0:T(512)S(1)}, u32[]{:S(2)}) copy-start(s32[384]{0:T(512)S(1)} %reshape.1035) | copy-start | bytes 4612
  30.9 3.1 %copy-start.17 = (pred[8,4,8]{2,1,0:T(4,128)(4,1)}, pred[8,4,8]{2,1,0:T(4,128)(4,1)S(1)}, u32[]{:S(2)}) copy-start(pred[8,4,8]{2,1,0:T(4,128)(4,1)S(1)} %broadcast_and_fusion) | copy-start | bytes 772
  46.3 35.7 %copy-start.24 = (bf16[4]{0:T(256)(128)(2,1)S(1)}, bf16[4]{0:T(256)(128)(2,1)}, u32[]{:S(2)}) copy-start(bf16[4]{0:T(256)(128)(2,1)} %fusion.51) | copy-start | bytes 28
  48.9 4.1 %collective-permute-start.8 = (bf16[4,1,48,128]{3,2,0,1:T(8,128)(2,1)S(1)}, bf16[4,1,48,128]{3,2,0,1:T(8,128)(2,1)S(1)}, u32[]{:S(2)}, u32[]{:S(2)}) collective-permute-start(bf16[4,1,48,128]{3,2,0,1:T(8,128)(2,1)S(1)} %pad_maximum_fusion.3), channel_id=1, source_target_pairs={{0,6},{1,7},{2,0},{3,1},{4,2},{5,3},{6,4},{7,5},{8,14},{9,15},{10,... | collective-permute-start | bytes 147464 | tf_op jit(solution)/shard_map/ppermute | solution.py:42
  53.0 11.7 %collective-permute-start.13 = (bf16[4,1,48,128]{3,2,0,1:T(8,128)(2,1)S(1)}, bf16[4,1,48,128]{3,2,0,1:T(8,128)(2,1)S(1)}, u32[]{:S(2)}, u32[]{:S(2)}) collective-permute-start(bf16[4,1,48,128]{3,2,0,1:T(8,128)(2,1)S(1)} %pad_maximum_fusion.3), channel_id=1, source_target_pairs={{0,1},{1,2},{2,3},{3,4},{4,5},{5,6},{6,7},{7,0},{8,9},{9,10},{10,1... | collective-permute-start | bytes 147464 | tf_op jit(solution)/shard_map/ppermute | solution.py:42
  53.7 52.7 %collective-permute-start.1 = (f32[4,1,48,128]{3,1,2,0:T(1,128)}, f32[4,1,48,128]{3,1,2,0:T(1,128)}, u32[]{:S(2)}, u32[]{:S(2)}) collective-permute-start(f32[4,1,48,128]{3,1,2,0:T(1,128)} %squeeze.114), channel_id=1, source_target_pairs={{0,2},{1,3},{2,4},{3,5},{4,6},{5,7},{6,0},{7,1},{8,10},{9,11},{10,... | collective-permute-start | bytes 294920 | tf_op jit(solution)/shard_map/ppermute | solution.py:42
  55.5 52.4 %collective-permute-start.2 = (f32[4,1,48,128]{3,1,2,0:T(1,128)}, f32[4,1,48,128]{3,1,2,0:T(1,128)}, u32[]{:S(2)}, u32[]{:S(2)}) collective-permute-start(f32[4,1,48,128]{3,1,2,0:T(1,128)} %squeeze.115), channel_id=1, source_target_pairs={{0,3},{1,4},{2,5},{3,6},{4,7},{5,0},{6,1},{7,2},{8,11},{9,12},{10,... | collective-permute-start | bytes 294920 | tf_op jit(solution)/shard_map/ppermute | solution.py:42
  60.1 48.4 %collective-permute-start.3 = (f32[4,1,48,128]{3,1,2,0:T(1,128)}, f32[4,1,48,128]{3,1,2,0:T(1,128)}, u32[]{:S(2)}, u32[]{:S(2)}) collective-permute-start(f32[4,1,48,128]{3,1,2,0:T(1,128)} %squeeze.116), channel_id=1, source_target_pairs={{0,4},{1,5},{2,6},{3,7},{4,0},{5,1},{6,2},{7,3},{8,12},{9,13},{10,... | collective-permute-start | bytes 294920 | tf_op jit(solution)/shard_map/ppermute | solution.py:42
  62.5 47.4 %collective-permute-start.4 = (f32[4,1,48,128]{3,1,2,0:T(1,128)}, f32[4,1,48,128]{3,1,2,0:T(1,128)}, u32[]{:S(2)}, u32[]{:S(2)}) collective-permute-start(f32[4,1,48,128]{3,1,2,0:T(1,128)} %squeeze.117), channel_id=1, source_target_pairs={{0,5},{1,6},{2,7},{3,0},{4,1},{5,2},{6,3},{7,4},{8,13},{9,14},{10,... | collective-permute-start | bytes 294920 | tf_op jit(solution)/shard_map/ppermute | solution.py:42
  64.8 47.2 %collective-permute-start.5 = (f32[4,1,48,128]{3,1,2,0:T(1,128)}, f32[4,1,48,128]{3,1,2,0:T(1,128)}, u32[]{:S(2)}, u32[]{:S(2)}) collective-permute-start(f32[4,1,48,128]{3,1,2,0:T(1,128)} %squeeze.118), channel_id=1, source_target_pairs={{0,6},{1,7},{2,0},{3,1},{4,2},{5,3},{6,4},{7,5},{8,14},{9,15},{10,... | collective-permute-start | bytes 294920 | tf_op jit(solution)/shard_map/ppermute | solution.py:42
  86.9 1.1 copy-start.6
  91.2 1.3 copy-start.29
  100.5 2.8 %copy-start.12 = (f32[48,8,7,128]{3,1,2,0:T(8,128)S(1)}, f32[48,8,7,128]{3,1,2,0:T(8,128)}, u32[]{:S(2)}) copy-start(f32[48,8,7,128]{3,1,2,0:T(8,128)} %get-tuple-element.123) | copy-start | bytes 4128772
  103.3 1.7 copy-start.11
  105.0 1.4 copy-start.16
  105.0 2.9 %copy-start.15 = (f32[4,1,48,128]{3,1,2,0:T(1,128)S(1)}, f32[4,1,48,128]{3,1,2,0:T(1,128)}, u32[]{:S(2)}) copy-start(f32[4,1,48,128]{3,1,2,0:T(1,128)} %squeeze.113) | copy-start | bytes 294916
  106.4 8.8 %collective-permute-start.6 = (f32[4,1,48,128]{3,1,2,0:T(1,128)S(1)}, f32[4,1,48,128]{3,1,2,0:T(1,128)S(1)}, u32[]{:S(2)}, u32[]{:S(2)}) collective-permute-start(f32[4,1,48,128]{3,1,2,0:T(1,128)S(1)} %copy-done.16), channel_id=1, source_target_pairs={{0,7},{1,0},{2,1},{3,2},{4,3},{5,4},{6,5},{7,6},{8,15},{9,8},{10,9... | collective-permute-start | bytes 294920 | tf_op jit(solution)/shard_map/ppermute | solution.py:42
  107.9 7.3 %collective-permute-start = (f32[4,1,48,128]{3,1,2,0:T(1,128)S(1)}, f32[4,1,48,128]{3,1,2,0:T(1,128)S(1)}, u32[]{:S(2)}, u32[]{:S(2)}) collective-permute-start(f32[4,1,48,128]{3,1,2,0:T(1,128)S(1)} %copy-done.15), channel_id=1, source_target_pairs={{0,1},{1,2},{2,3},{3,4},{4,5},{5,6},{6,7},{7,0},{8,9},{9,10},{10,1... | collective-permute-start | bytes 294920 | tf_op jit(solution)/shard_map/ppermute | solution.py:42
  108.5 20.9 %collective-permute-start.26 = (bf16[4,1,48,128]{3,2,0,1:T(8,128)(2,1)S(1)}, bf16[4,1,48,128]{3,2,0,1:T(8,128)(2,1)}, u32[]{:S(2)}, u32[]{:S(2)}) collective-permute-start(bf16[4,1,48,128]{3,2,0,1:T(8,128)(2,1)S(1)} %pad_maximum_fusion.4), channel_id=1, source_target_pairs={{0,2},{1,3},{2,4},{3,5},{4,6},{5,7},{6,0},{7,1},{8,10},{9,11},{10,... | collective-permute-start | bytes 147464 | tf_op jit(solution)/shard_map/ppermute | solution.py:42
  109.9 18.7 %collective-permute-start.25 = (bf16[4,1,48,128]{3,2,0,1:T(8,128)(2,1)S(1)}, bf16[4,1,48,128]{3,2,0,1:T(8,128)(2,1)}, u32[]{:S(2)}, u32[]{:S(2)}) collective-permute-start(bf16[4,1,48,128]{3,2,0,1:T(8,128)(2,1)S(1)} %pad_maximum_fusion.4), channel_id=1, source_target_pairs={{0,3},{1,4},{2,5},{3,6},{4,7},{5,0},{6,1},{7,2},{8,11},{9,12},{10,... | collective-permute-start | bytes 147464 | tf_op jit(solution)/shard_map/ppermute | solution.py:42
  112.0 15.8 %collective-permute-start.24 = (bf16[4,1,48,128]{3,2,0,1:T(8,128)(2,1)S(1)}, bf16[4,1,48,128]{3,2,0,1:T(8,128)(2,1)}, u32[]{:S(2)}, u32[]{:S(2)}) collective-permute-start(bf16[4,1,48,128]{3,2,0,1:T(8,128)(2,1)S(1)} %pad_maximum_fusion.4), channel_id=1, source_target_pairs={{0,4},{1,5},{2,6},{3,7},{4,0},{5,1},{6,2},{7,3},{8,12},{9,13},{10,... | collective-permute-start | bytes 147464 | tf_op jit(solution)/shard_map/ppermute | solution.py:42
  115.2 11.8 %collective-permute-start.23 = (bf16[4,1,48,128]{3,2,0,1:T(8,128)(2,1)S(1)}, bf16[4,1,48,128]{3,2,0,1:T(8,128)(2,1)}, u32[]{:S(2)}, u32[]{:S(2)}) collective-permute-start(bf16[4,1,48,128]{3,2,0,1:T(8,128)(2,1)S(1)} %pad_maximum_fusion.4), channel_id=1, source_target_pairs={{0,5},{1,6},{2,7},{3,0},{4,1},{5,2},{6,3},{7,4},{8,13},{9,14},{10,... | collective-permute-start | bytes 147464 | tf_op jit(solution)/shard_map/ppermute | solution.py:42
  115.2 5.1 %collective-permute-start.21 = (bf16[4,1,48,128]{3,2,0,1:T(8,128)(2,1)S(1)}, bf16[4,1,48,128]{3,2,0,1:T(8,128)(2,1)}, u32[]{:S(2)}, u32[]{:S(2)}) collective-permute-start(bf16[4,1,48,128]{3,2,0,1:T(8,128)(2,1)S(1)} %pad_maximum_fusion.4), channel_id=1, source_target_pairs={{0,7},{1,0},{2,1},{3,2},{4,3},{5,4},{6,5},{7,6},{8,15},{9,8},{10,9... | collective-permute-start | bytes 147464 | tf_op jit(solution)/shard_map/ppermute | solution.py:42
  118.9 20.4 %copy-start.8 = (f32[48,8,7,128]{3,0,2,1:T(8,128)S(1)}, f32[48,8,7,128]{3,0,2,1:T(8,128)}, u32[]{:S(2)}) copy-start(f32[48,8,7,128]{3,0,2,1:T(8,128)} %copy.139) | copy-start | bytes 4128772
  120.4 4.1 %collective-permute-start.22 = (bf16[4,1,48,128]{3,2,0,1:T(8,128)(2,1)S(1)}, bf16[4,1,48,128]{3,2,0,1:T(8,128)(2,1)S(1)}, u32[]{:S(2)}, u32[]{:S(2)}) collective-permute-start(bf16[4,1,48,128]{3,2,0,1:T(8,128)(2,1)S(1)} %pad_maximum_fusion.4), channel_id=1, source_target_pairs={{0,6},{1,7},{2,0},{3,1},{4,2},{5,3},{6,4},{7,5},{8,14},{9,15},{10,... | collective-permute-start | bytes 147464 | tf_op jit(solution)/shard_map/ppermute | solution.py:42
  124.5 8.0 %collective-permute-start.27 = (bf16[4,1,48,128]{3,2,0,1:T(8,128)(2,1)S(1)}, bf16[4,1,48,128]{3,2,0,1:T(8,128)(2,1)S(1)}, u32[]{:S(2)}, u32[]{:S(2)}) collective-permute-start(bf16[4,1,48,128]{3,2,0,1:T(8,128)(2,1)S(1)} %pad_maximum_fusion.4), channel_id=1, source_target_pairs={{0,1},{1,2},{2,3},{3,4},{4,5},{5,6},{6,7},{7,0},{8,9},{9,10},{10,1... | collective-permute-start | bytes 147464 | tf_op jit(solution)/shard_map/ppermute | solution.py:42
  144.7 1.8 copy-start.13
  144.7 1.9 copy-start.14
  146.7 7.3 %copy-start.7 = (bf16[1,50,50,128]{3,0,2,1:T(2,128)(2,1)S(1)}, bf16[1,50,50,128]{3,0,2,1:T(2,128)(2,1)}, u32[]{:S(2)}) copy-start(bf16[1,50,50,128]{3,0,2,1:T(2,128)(2,1)} %copy-done.6) | copy-start | bytes 1920004
  146.7 7.3 %copy-start.10 = (bf16[1,48,48,128]{3,1,2,0:T(8,128)(2,1)S(1)}, bf16[1,48,48,128]{3,1,2,0:T(8,128)(2,1)}, u32[]{:S(2)}) copy-start(bf16[1,48,48,128]{3,1,2,0:T(8,128)(2,1)} %copy-done.9) | copy-start | bytes 1769476
  154.0 7.8 %copy-start.5 = (f32[1,50,50,128]{3,1,2,0:T(8,128)S(1)}, f32[1,50,50,128]{3,1,2,0:T(8,128)}, u32[]{:S(2)}) copy-start(f32[1,50,50,128]{3,1,2,0:T(8,128)} %slice_bitcast_fusion) | copy-start | bytes 3840004
  161.7 2.1 collective-permute-start.28
  163.8 9.3 %copy-start.23 = (f32[4]{0:T(128)S(1)}, f32[4]{0:T(128)}, u32[]{:S(2)}) copy-start(f32[4]{0:T(128)} %copy-done.22) | copy-start | bytes 52
  163.9 14.5 %copy-start.20 = (f32[4,48]{1,0:T(4,128)S(1)}, f32[4,48]{1,0:T(4,128)}, u32[]{:S(2)}) copy-start(f32[4,48]{1,0:T(4,128)} %constant.263.clone) | copy-start | bytes 2308
  163.9 9.1 %collective-permute-start.29 = (f32[73728]{0:T(1024)S(1)}, f32[73728]{0:T(1024)S(1)}, u32[]{:S(2)}, u32[]{:S(2)}) collective-permute-start(f32[73728]{0:T(1024)S(1)} %slice_select_fusion), channel_id=1, source_target_pairs={{0,16},{8,24},{16,0},{24,8},{1,17},{9,25},{17,1},{25,9},{2,18},{10... | collective-permute-start | bytes 884744 | tf_op jit(solution)/shard_map/ppermute | solution.py:158
  165.5 13.1 %copy-start.4 = (s32[384]{0:T(512)S(1)}, s32[384]{0:T(512)}, u32[]{:S(2)}) copy-start(s32[384]{0:T(512)} %copy-done.3) | copy-start | bytes 4612
  173.1 5.2 %collective-permute-start.30 = (f32[36864]{0:T(1024)S(1)}, f32[36864]{0:T(1024)S(1)}, u32[]{:S(2)}, u32[]{:S(2)}) collective-permute-start(f32[36864]{0:T(1024)S(1)} %slice_select_fusion.1), channel_id=1, source_target_pairs={{0,1},{1,0},{2,3},{3,2},{4,5},{5,4},{6,7},{7,6},{8,9},{9,8},{10,11... | collective-permute-start | bytes 442376 | tf_op jit(solution)/shard_map/ppermute | solution.py:158
  178.3 4.4 %collective-permute-start.31 = (f32[18432]{0:T(1024)S(1)}, f32[18432]{0:T(1024)S(1)}, u32[]{:S(2)}, u32[]{:S(2)}) collective-permute-start(f32[18432]{0:T(1024)S(1)} %slice_select_fusion.2), channel_id=1, source_target_pairs={{0,2},{1,3},{2,0},{3,1},{4,6},{5,7},{6,4},{7,5},{8,10},{9,11},{10,... | collective-permute-start | bytes 221192 | tf_op jit(solution)/shard_map/ppermute | solution.py:158
  178.5 6.2 %copy-start.18 = (pred[8,4,8]{2,1,0:T(4,128)(4,1)S(1)}, pred[8,4,8]{2,1,0:T(4,128)(4,1)}, u32[]{:S(2)}) copy-start(pred[8,4,8]{2,1,0:T(4,128)(4,1)} %copy-done.17) | copy-start | bytes 772
  182.8 4.9 %collective-permute-start.32 = (f32[9216]{0:T(1024)S(1)}, f32[9216]{0:T(1024)S(1)}, u32[]{:S(2)}, u32[]{:S(2)}) collective-permute-start(f32[9216]{0:T(1024)S(1)} %slice_select_fusion.3), channel_id=1, source_target_pairs={{0,4},{1,5},{2,6},{3,7},{4,0},{5,1},{6,2},{7,3},{8,12},{9,13},{10,... | collective-permute-start | bytes 110600 | tf_op jit(solution)/shard_map/ppermute | solution.py:158
  187.7 7.5 %collective-permute-start.33 = (f32[9216]{0:T(1024)S(1)}, f32[9216]{0:T(1024)S(1)}, u32[]{:S(2)}, u32[]{:S(2)}) collective-permute-start(f32[9216]{0:T(1024)S(1)} %select_add_fusion.3), channel_id=1, source_target_pairs={{0,4},{1,5},{2,6},{3,7},{4,0},{5,1},{6,2},{7,3},{8,12},{9,13},{10,... | collective-permute-start | bytes 110600 | tf_op jit(solution)/shard_map/ppermute | solution.py:158
  191.4 11.2 %collective-permute-start.15 = (f32[4,1,48,128]{3,1,2,0:T(1,128)}, f32[4,1,48,128]{3,1,2,0:T(1,128)}, u32[]{:S(2)}, u32[]{:S(2)}) collective-permute-start(f32[4,1,48,128]{3,1,2,0:T(1,128)} %squeeze.129), channel_id=1, source_target_pairs={{0,2},{1,3},{2,4},{3,5},{4,6},{5,7},{6,0},{7,1},{8,10},{9,11},{10,... | collective-permute-start | bytes 294920 | tf_op jit(solution)/shard_map/ppermute | solution.py:42
  191.8 11.2 %collective-permute-start.16 = (f32[4,1,48,128]{3,1,2,0:T(1,128)}, f32[4,1,48,128]{3,1,2,0:T(1,128)}, u32[]{:S(2)}, u32[]{:S(2)}) collective-permute-start(f32[4,1,48,128]{3,1,2,0:T(1,128)} %squeeze.130), channel_id=1, source_target_pairs={{0,3},{1,4},{2,5},{3,6},{4,7},{5,0},{6,1},{7,2},{8,11},{9,12},{10,... | collective-permute-start | bytes 294920 | tf_op jit(solution)/shard_map/ppermute | solution.py:42
  195.8 9.0 %collective-permute-start.34 = (f32[18432]{0:T(1024)}, f32[18432]{0:T(1024)}, u32[]{:S(2)}, u32[]{:S(2)}) collective-permute-start(f32[18432]{0:T(1024)} %maximum_select_fusion.4), channel_id=1, source_target_pairs={{0,2},{1,3},{2,0},{3,1},{4,6},{5,7},{6,4},{7,5},{8,10},{9,11},{10,... | collective-permute-start | bytes 221192 | tf_op jit(solution)/shard_map/ppermute | solution.py:158
  198.1 9.0 %collective-permute-start.17 = (f32[4,1,48,128]{3,1,2,0:T(1,128)}, f32[4,1,48,128]{3,1,2,0:T(1,128)S(1)}, u32[]{:S(2)}, u32[]{:S(2)}) collective-permute-start(f32[4,1,48,128]{3,1,2,0:T(1,128)} %squeeze.131), channel_id=1, source_target_pairs={{0,4},{1,5},{2,6},{3,7},{4,0},{5,1},{6,2},{7,3},{8,12},{9,13},{10,... | collective-permute-start | bytes 294920 | tf_op jit(solution)/shard_map/ppermute | solution.py:42
  199.3 9.1 %collective-permute-start.18 = (f32[4,1,48,128]{3,1,2,0:T(1,128)S(1)}, f32[4,1,48,128]{3,1,2,0:T(1,128)S(1)}, u32[]{:S(2)}, u32[]{:S(2)}) collective-permute-start(f32[4,1,48,128]{3,1,2,0:T(1,128)S(1)} %squeeze.132), channel_id=1, source_target_pairs={{0,5},{1,6},{2,7},{3,0},{4,1},{5,2},{6,3},{7,4},{8,13},{9,14},{10,... | collective-permute-start | bytes 294920 | tf_op jit(solution)/shard_map/ppermute | solution.py:42
  202.5 5.9 %collective-permute-start.19 = (f32[4,1,48,128]{3,1,2,0:T(1,128)S(1)}, f32[4,1,48,128]{3,1,2,0:T(1,128)S(1)}, u32[]{:S(2)}, u32[]{:S(2)}) collective-permute-start(f32[4,1,48,128]{3,1,2,0:T(1,128)S(1)} %squeeze.133), channel_id=1, source_target_pairs={{0,6},{1,7},{2,0},{3,1},{4,2},{5,3},{6,4},{7,5},{8,14},{9,15},{10,... | collective-permute-start | bytes 294920 | tf_op jit(solution)/shard_map/ppermute | solution.py:42
  202.9 5.7 %collective-permute-start.20 = (f32[4,1,48,128]{3,1,2,0:T(1,128)S(1)}, f32[4,1,48,128]{3,1,2,0:T(1,128)S(1)}, u32[]{:S(2)}, u32[]{:S(2)}) collective-permute-start(f32[4,1,48,128]{3,1,2,0:T(1,128)S(1)} %squeeze.134), channel_id=1, source_target_pairs={{0,7},{1,0},{2,1},{3,2},{4,3},{5,4},{6,5},{7,6},{8,15},{9,8},{10,9... | collective-permute-start | bytes 294920 | tf_op jit(solution)/shard_map/ppermute | solution.py:42
  204.8 7.6 %collective-permute-start.14 = (f32[4,1,48,128]{3,1,2,0:T(1,128)}, f32[4,1,48,128]{3,1,2,0:T(1,128)S(1)}, u32[]{:S(2)}, u32[]{:S(2)}) collective-permute-start(f32[4,1,48,128]{3,1,2,0:T(1,128)} %squeeze.128), channel_id=1, source_target_pairs={{0,1},{1,2},{2,3},{3,4},{4,5},{5,6},{6,7},{7,0},{8,9},{9,10},{10,1... | collective-permute-start | bytes 294920 | tf_op jit(solution)/shard_map/ppermute | solution.py:42
  207.1 6.3 %collective-permute-start.35 = (f32[36864]{0:T(1024)S(1)}, f32[36864]{0:T(1024)S(1)}, u32[]{:S(2)}, u32[]{:S(2)}) collective-permute-start(f32[36864]{0:T(1024)S(1)} %maximum_select_fusion.3), channel_id=1, source_target_pairs={{0,1},{1,0},{2,3},{3,2},{4,5},{5,4},{6,7},{7,6},{8,9},{9,8},{10,11... | collective-permute-start | bytes 442376 | tf_op jit(solution)/shard_map/ppermute | solution.py:158
  213.5 6.9 %collective-permute-start.36 = (f32[73728]{0:T(1024)S(1)}, f32[73728]{0:T(1024)}, u32[]{:S(2)}, u32[]{:S(2)}) collective-permute-start(f32[73728]{0:T(1024)S(1)} %maximum_select_fusion.2), channel_id=1, source_target_pairs={{0,16},{8,24},{16,0},{24,8},{1,17},{9,25},{17,1},{25,9},{2,18},{10... | collective-permute-start | bytes 884744 | tf_op jit(solution)/shard_map/ppermute | solution.py:158
  221.5 2.1 collective-permute-start.37
  (4 other events, 3.5 us)
